TPU v7x, 256 devices: a whole 4x4x8 slice. The times are simulated.
256 devices in a mesh: ctx: 32 (over x, y, core), tp: 8 (over z).
Axes of the slice: x: 4, y: 4, z: 8, core: 2. Of those that a mesh axis runs over, the one named last changes fastest.
Arguments:
- hidden_states: bfloat16 [65536, 4096], P('ctx', 'tp')
- chosen: int32 [12288], P('ctx'), may hold values from 0 to 2048, as said below
- router_gate: float32 [12288], P('ctx'), may hold values from 0.2 to 1
- w_query: bfloat16 [4096, 4096], P(None, 'tp'), may hold values from -0.09375 to 0.09375
- w_key: bfloat16 [4096, 1024], P(None, 'tp'), may hold values from -0.09375 to 0.09375
- w_value: bfloat16 [4096, 1024], P(None, 'tp'), may hold values from -0.09375 to 0.09375
Outputs:
- attended: bfloat16 [12288, 4096], P('ctx', 'tp')
Inputs may be any that keep to these rules, and one draw needn't show every extreme that they name: `chosen`: each shard's 384 slots hold the sorted distinct positions of its routed tokens, then 2048 in every unused slot; a shard routes from 128 to 384 tokens, some shard exactly 384, and all shards together 65536 // 8.
All inputs are finite; a program needn't handle non-finite values.
Results may differ from a plain program's by a relative error of at most 0.035.
Values may be sent and summed in bfloat16 or wider, within the bound.
No kernel may reach another device: no remote copies, remote signals or barrier semaphores. Data moves between devices by JAX's collectives and lax.ppermute only.
A program may use at most 64 MiB of HBM per device.

v0:
```python
import functools
import math

import jax
import jax.numpy as jnp
from jax import lax
from jax.experimental import pallas as pl
from jax.experimental.pallas import tpu as pltpu
from jax.sharding import PartitionSpec as P

HEAD_DIM = 128


ROPE_BASE = 500000.0
MASKED = -1e30
SUB = 128


def rotate(values_in, position):
    half_dim = values_in.shape[-1] // 2
    frequency = jnp.exp(
        jnp.arange(half_dim, dtype=jnp.float32) * (-2.0 * math.log(ROPE_BASE) / values_in.shape[-1])
    )
    angles = position.astype(jnp.float32)[:, None] * frequency[None, :]
    cosine = jnp.cos(angles)[:, None, :]
    sine = jnp.sin(angles)[:, None, :]
    first = values_in[..., :half_dim]
    second = values_in[..., half_dim:]
    return jnp.concatenate(
        [first * cosine - second * sine, second * cosine + first * sine], axis=-1
    )


def attend_kernel(scalars, q_ref, qpos_ref, kpos_ref, kv_ref, acc_ref, m_ref, l_ref, *, cols, steps):
    i = pl.program_id(0)
    first = scalars[0]
    active = i < scalars[1]
    q_blocks = scalars[2]
    diagonal_shard = scalars[3]
    t = first + i
    count = scalars[4 + jnp.minimum(t, scalars.shape[0] - 5)]
    key_blocks = (count + (SUB - 1)) // SUB
    head_dim = q_ref.shape[0]
    pieces = kv_ref.shape[1] // SUB

    @pl.when(i == 0)
    def _():
        m_ref[...] = jnp.full(m_ref.shape, MASKED, jnp.float32)
        l_ref[...] = jnp.zeros(l_ref.shape, jnp.float32)
        acc_ref[...] = jnp.zeros(acc_ref.shape, jnp.float32)

    def step(qb, width, diagonal):
        c0 = qb * cols
        q = q_ref[:, c0:c0 + cols]
        chunks = [
            jnp.dot(kv_ref[0:SUB, j * SUB:(j + 1) * SUB], q, preferred_element_type=jnp.float32)
            for j in range(width // SUB)
        ]
        if diagonal:
            masks = [kpos_ref[j * SUB:(j + 1) * SUB, :] <= qpos_ref[:, c0:c0 + cols] for j in range(len(chunks))]
        else:
            last = lax.broadcasted_iota(jnp.int32, chunks[-1].shape, 0) + (width - SUB) < count
            masks = [None] * (len(chunks) - 1) + [last]
        m_prev = m_ref[:, c0:c0 + cols]
        m_new = m_prev
        for chunk, mask in zip(chunks, masks):
            kept = chunk if mask is None else jnp.where(mask, chunk, MASKED)
            m_new = jnp.maximum(m_new, jnp.max(kept, axis=0, keepdims=True))
        alpha = jnp.exp(m_prev - m_new)
        weights = []
        for chunk, mask in zip(chunks, masks):
            w = jnp.exp(chunk - m_new)
            weights.append(w if mask is None else jnp.where(mask, w, 0.0))
        p = jnp.concatenate(weights, axis=0)
        l_ref[:, c0:c0 + cols] = alpha * l_ref[:, c0:c0 + cols] + jnp.sum(p, axis=0, keepdims=True)
        acc_ref[:, c0:c0 + cols] = alpha * acc_ref[:, c0:c0 + cols] + jnp.dot(
            kv_ref[SUB:SUB + head_dim, 0:width], p.astype(jnp.bfloat16), preferred_element_type=jnp.float32
        )
        m_ref[:, c0:c0 + cols] = m_new

    for qb in range(q_ref.shape[1] // cols):
        for blocks in range(1, pieces + 1):
            for diagonal in (False, True):
                hit = (t == diagonal_shard) if diagonal else (t != diagonal_shard)

                @pl.when(active & hit & (qb < q_blocks) & (key_blocks == blocks))
                def _():
                    step(qb, blocks * SUB, diagonal)


def attend(scalars, q, qpos, kpos, kv, steps, interpret=False):
    head_dim, q_rows = q.shape
    shards, kv_rows, slots = kv.shape
    cols = kpos.shape[1]
    kernel = functools.partial(attend_kernel, cols=cols, steps=steps)

    def fixed(i, sc):
        return (0, 0)

    def shard_of(i, sc):
        last = jnp.maximum(sc[1] - 1, 0)
        return (jnp.clip(sc[0] + jnp.minimum(i, last), 0, shards - 1), 0, 0)

    grid_spec = pltpu.PrefetchScalarGridSpec(
        num_scalar_prefetch=1,
        grid=(steps,),
        in_specs=[
            pl.BlockSpec((head_dim, q_rows), fixed),
            pl.BlockSpec((1, q_rows), fixed),
            pl.BlockSpec((slots, cols), fixed),
            pl.BlockSpec((None, SUB + head_dim, slots), shard_of),
        ],
        out_specs=[
            pl.BlockSpec((head_dim, q_rows), fixed),
            pl.BlockSpec((1, q_rows), fixed),
            pl.BlockSpec((1, q_rows), fixed),
        ],
    )
    return pl.pallas_call(
        kernel,
        grid_spec=grid_spec,
        out_shape=[
            jax.ShapeDtypeStruct((head_dim, q_rows), jnp.float32),
            jax.ShapeDtypeStruct((1, q_rows), jnp.float32),
            jax.ShapeDtypeStruct((1, q_rows), jnp.float32),
        ],
        compiler_params=pltpu.CompilerParams(dimension_semantics=("arbitrary",)),
        interpret=interpret,
    )(scalars, q, qpos, kpos, kv)


def merge(first, second):
    acc_a, m_a, l_a = first
    acc_b, m_b, l_b = second
    m_a = jnp.where(l_a > 0.0, m_a, MASKED)
    m_b = jnp.where(l_b > 0.0, m_b, MASKED)
    m = jnp.maximum(m_a, m_b)
    scale_a = jnp.exp(m_a - m)
    scale_b = jnp.exp(m_b - m)
    return acc_a * scale_a + acc_b * scale_b, l_a * scale_a + l_b * scale_b


FLAG_ROWS = 16
EXTRA_OWN = 1


def pack_payload(key_rows, value_rows, live):
    slot_count = live.shape[0]
    head_dim = key_rows.shape[-1]
    keys = key_rows.reshape(slot_count // SUB, SUB, head_dim)
    keys = jnp.transpose(keys, (1, 0, 2)).reshape(SUB, slot_count)
    values = jnp.transpose(value_rows.reshape(slot_count, head_dim))
    flags = jnp.zeros((FLAG_ROWS, slot_count), jnp.bfloat16).at[0].set(live.astype(jnp.bfloat16))
    return jnp.concatenate([keys, values, flags], axis=0)


def ring_project(picked, weights, axis):
    size = lax.axis_size(axis)
    idx = lax.axis_index(axis)
    width = picked.shape[1]
    forward = [(i, (i + 1) % size) for i in range(size)]
    backward = [(i, (i - 1) % size) for i in range(size)]

    def partial(block, source):
        start = source * width
        return [
            jnp.dot(block, lax.dynamic_slice_in_dim(w, start, width, axis=0), preferred_element_type=jnp.float32)
            for w in weights
        ]

    sums = partial(picked, idx)
    ahead = picked
    behind = picked
    steps_behind = (size - 1) // 2
    for step in range(1, steps_behind + 1):
        ahead = lax.ppermute(ahead, axis, forward)
        behind = lax.ppermute(behind, axis, backward)
        for part in (partial(ahead, (idx - step) % size), partial(behind, (idx + step) % size)):
            sums = [s + p for s, p in zip(sums, part)]
    if size % 2 == 0:
        rows = picked.shape[0] // 2
        top = lax.ppermute(ahead[:rows], axis, forward)
        bottom = lax.ppermute(behind[rows:], axis, backward)
        part = partial(jnp.concatenate([top, bottom], axis=0), (idx + size // 2) % size)
        sums = [s + p for s, p in zip(sums, part)]
    return sums


def body(hidden_states, chosen, router_gate, w_query, w_key, w_value):
    seq_rows = hidden_states.shape[0]
    slot_count = chosen.shape[0]
    head_dim = HEAD_DIM
    query_width = w_query.shape[1]
    kv_width = w_key.shape[1]
    kv_local = kv_width // head_dim
    heads_local = query_width // head_dim
    group = heads_local // kv_local
    shards = lax.axis_size("ctx")
    live = chosen < seq_rows
    pad_mark = shards * seq_rows + 1
    position = jnp.where(live, lax.axis_index("ctx") * seq_rows + chosen, pad_mark)
    picked = hidden_states[jnp.minimum(chosen, seq_rows - 1)]
    gated = jnp.where(live, router_gate, 0.0)
    query_part, key_part, value_part = ring_project(picked, (w_query, w_key, w_value), "tp")
    queries = (
        rotate(query_part.reshape(slot_count, heads_local, head_dim), position) * head_dim ** (-0.5)
    ).astype(jnp.bfloat16)
    key_rows = rotate(key_part.reshape(slot_count, kv_local, head_dim), position).astype(
        jnp.bfloat16
    )
    value_rows = value_part.reshape(slot_count, kv_local, head_dim).astype(jnp.bfloat16)
    payload = pack_payload(key_rows, value_rows, live)
    payload = lax.all_gather(payload, "ctx", axis=0, tiled=True)
    blocks = payload.reshape(shards, payload.shape[0] // shards, slot_count)
    flag_row = blocks.shape[1] - FLAG_ROWS
    counts = jnp.sum(blocks[:, flag_row, :].astype(jnp.float32), axis=1).astype(jnp.int32)
    own = lax.axis_index("ctx")
    half = shards // 2
    partner = shards - 1 - own

    def live_blocks(count):
        return (count + (SUB - 1)) // SUB

    def scalars_of(first, count, q_blocks, diagonal):
        head = jnp.stack([first, count, q_blocks, diagonal]).astype(jnp.int32)
        return jnp.concatenate([head, counts])

    q_tiles = slot_count // SUB
    flat_q = jnp.transpose(
        queries.reshape(q_tiles, SUB, group, head_dim), (0, 2, 1, 3)
    ).reshape(slot_count * group, head_dim)
    own_q = jnp.transpose(flat_q)

    def per_column(values):
        spread = jnp.broadcast_to(values.reshape(q_tiles, 1, SUB), (q_tiles, group, SUB))
        return spread.reshape(1, slot_count * group)

    own_pos = jnp.broadcast_to(chosen[:, None], (slot_count, group * SUB))
    query_pos = per_column(chosen)
    guest_q = lax.ppermute(own_q, "ctx", [(j, shards - 1 - j) for j in range(half, shards)])
    guest_count = jnp.maximum(half - EXTRA_OWN - own, 0)
    guest_scalars = scalars_of(
        jnp.int32(0), guest_count, live_blocks(counts[partner]), jnp.int32(-1)
    )

    def guest_work(q):
        return tuple(attend(guest_scalars, q, query_pos, own_pos, blocks, half - EXTRA_OWN))

    def no_guest(q):
        rows = (1, q.shape[1])
        return (
            jnp.zeros(q.shape, jnp.float32),
            jnp.full(rows, MASKED, jnp.float32),
            jnp.zeros(rows, jnp.float32),
        )

    guest_state = lax.cond(guest_count > 0, guest_work, no_guest, guest_q)
    returned = lax.ppermute(guest_state, "ctx", [(j, shards - 1 - j) for j in range(half)])
    own_q, guest_state = lax.optimization_barrier((own_q, guest_state))
    own_first = jnp.maximum(own - (half - 1) - EXTRA_OWN, 0)
    own_scalars = scalars_of(
        own_first, own - own_first + 1, live_blocks(jnp.sum(live.astype(jnp.int32))), own
    )
    own_state = tuple(attend(own_scalars, own_q, query_pos, own_pos, blocks, half + EXTRA_OWN))
    acc, total = merge(own_state, returned)
    out = (acc / jnp.where(total > 0.0, total, 1.0)) * per_column(gated)
    out = jnp.transpose(out.astype(jnp.bfloat16))
    out = jnp.transpose(out.reshape(q_tiles, group, SUB, head_dim), (0, 2, 1, 3))
    return out.reshape(slot_count, query_width)


def solution(mesh):
    placed = (P("ctx", "tp"), P("ctx"), P("ctx"), P(None, "tp"), P(None, "tp"), P(None, "tp"))
    return jax.shard_map(
        body, mesh=mesh, in_specs=placed, out_specs=P("ctx", "tp"), check_vma=False
    )
```

profile of v0, /device:TPU:31, one launch (start us, length us, event | category | flops | bytes accessed | tf_op | source)
XLA Modules:
  0.0 181.6 jit_solution(18406822073375337479)
XLA Ops:
  8.1 2.1 %gather_fusion = bf16[384,512]{1,0:T(8,128)(2,1)S(1)} fusion(bf16[2048,512]{1,0:T(8,128)(2,1)S(1)} %copy-done, s32[1024]{0:T(1024)S(1)} %pad_clamp_fusion), kind=kCustom, calls=%fused_computation | custom fusion | bytes 787968 | tf_op jit(solution)/shard_map/gather | solution.py:202
  10.2 1.7 collective-permute-start
  11.9 4.0 %collective-permute-start.1 = (bf16[384,512]{1,0:T(8,128)(2,1)S(1)}, bf16[384,512]{1,0:T(8,128)(2,1)S(1)}, u32[]{:S(2)}, u32[]{:S(2)}) collective-permute-start(bf16[384,512]{1,0:T(8,128)(2,1)S(1)} %gather_fusion), channel_id=1, source_target_pairs={{0,7},{1,0},{2,1},{3,2},{4,3},{5,4},{6,5},{7,6},{8,15},{9,8},{10,9... | collective-permute-start | bytes 1179656 | tf_op jit(solution)/shard_map/ppermute | solution.py:177
  17.4 1.3 fusion.40
  18.7 5.0 %collective-permute-done.1 = bf16[384,512]{1,0:T(8,128)(2,1)S(1)} collective-permute-done((bf16[384,512]{1,0:T(8,128)(2,1)S(1)}, bf16[384,512]{1,0:T(8,128)(2,1)S(1)}, u32[]{:S(2)}, u32[]{:S(2)}) %collective-permute-start.1) | collective-permute-done | bytes 393248 | tf_op jit(solution)/shard_map/ppermute | solution.py:177
  23.8 3.4 %collective-permute-start.3 = (bf16[384,512]{1,0:T(8,128)(2,1)S(1)}, bf16[384,512]{1,0:T(8,128)(2,1)S(1)}, u32[]{:S(2)}, u32[]{:S(2)}) collective-permute-start(bf16[384,512]{1,0:T(8,128)(2,1)S(1)} %collective-permute-done.1), channel_id=1, source_target_pairs={{0,7},{1,0},{2,1},{3,2},{4,3},{5,4},{6,5},{7,6},{8,15},{9,8},{10,9... | collective-permute-start | bytes 1179656 | tf_op jit(solution)/shard_map/ppermute | solution.py:177
  27.2 1.4 convolution_add_fusion.11
  29.7 1.2 convolution_add_fusion.10
  31.0 1.2 convolution_add_fusion.6
  32.2 5.0 %collective-permute-done.2 = bf16[384,512]{1,0:T(8,128)(2,1)S(1)} collective-permute-done((bf16[384,512]{1,0:T(8,128)(2,1)S(1)}, bf16[384,512]{1,0:T(8,128)(2,1)S(1)}, u32[]{:S(2)}, u32[]{:S(2)}) %collective-permute-start.2) | collective-permute-done | bytes 393248 | tf_op jit(solution)/shard_map/ppermute | solution.py:176
  37.3 2.7 %collective-permute-start.5 = (bf16[384,512]{1,0:T(8,128)(2,1)S(1)}, bf16[384,512]{1,0:T(8,128)(2,1)S(1)}, u32[]{:S(2)}, u32[]{:S(2)}) collective-permute-start(bf16[384,512]{1,0:T(8,128)(2,1)S(1)} %collective-permute-done.3), channel_id=1, source_target_pairs={{0,7},{1,0},{2,1},{3,2},{4,3},{5,4},{6,5},{7,6},{8,15},{9,8},{10,9... | collective-permute-start | bytes 1179656 | tf_op jit(solution)/shard_map/ppermute | solution.py:177
  41.9 4.5 %collective-permute-done.4 = bf16[384,512]{1,0:T(8,128)(2,1)S(1)} collective-permute-done((bf16[384,512]{1,0:T(8,128)(2,1)S(1)}, bf16[384,512]{1,0:T(8,128)(2,1)S(1)}, u32[]{:S(2)}, u32[]{:S(2)}) %collective-permute-start.4) | collective-permute-done | bytes 393248 | tf_op jit(solution)/shard_map/ppermute | solution.py:176
  46.6 2.9 %collective-permute-start.7 = (bf16[192,512]{1,0:T(8,128)(2,1)S(1)}, bf16[192,512]{1,0:T(8,128)(2,1)S(1)}, u32[]{:S(2)}, u32[]{:S(2)}) collective-permute-start(bf16[192,512]{1,0:T(8,128)(2,1)S(1)} %slice.45), channel_id=1, source_target_pairs={{0,7},{1,0},{2,1},{3,2},{4,3},{5,4},{6,5},{7,6},{8,15},{9,8},{10,9... | collective-permute-start | bytes 589832 | tf_op jit(solution)/shard_map/ppermute | solution.py:183
  50.1 2.2 %collective-permute-done.6 = bf16[192,512]{1,0:T(8,128)(2,1)S(1)} collective-permute-done((bf16[192,512]{1,0:T(8,128)(2,1)S(1)}, bf16[192,512]{1,0:T(8,128)(2,1)S(1)}, u32[]{:S(2)}, u32[]{:S(2)}) %collective-permute-start.6) | collective-permute-done | bytes 196640 | tf_op jit(solution)/shard_map/ppermute | solution.py:182
  56.3 1.4 concatenate.35
  59.4 1.6 copy.10
  61.0 1.4 fusion.10
  62.4 1.6 pad_maximum_fusion
  65.2 1.6 fusion.23
  66.8 1.5 convolution_add_fusion.3
  68.4 1.4 convolution_add_fusion.2
  71.4 1.3 fusion.2
  72.6 1.4 copy.15
  77.2 7.1 %collective-permute-start.8 = (bf16[128,1536]{1,0:T(8,128)(2,1)S(1)}, bf16[128,1536]{1,0:T(8,128)(2,1)}, u32[]{:S(2)}, u32[]{:S(2)}) collective-permute-start(bf16[128,1536]{1,0:T(8,128)(2,1)S(1)} %bitcast.71), channel_id=1, source_target_pairs={{128,120},{136,112},{144,104},{152,96},{160,88},{168,80},{176,72},... | collective-permute-start | bytes 1179656 | tf_op jit(solution)/shard_map/ppermute | solution.py:240
  84.3 39.1 %all-gather.2.cloned.1.call-done = bf16[8704,384]{1,0:T(8,128)(2,1)} async-done(((bf16[272,384]{1,0:T(8,128)(2,1)}), bf16[8704,384]{1,0:T(8,128)(2,1)}) %all-gather.2.cloned.1.call-update) | async-done | bytes 6684688 | tf_op jit(solution)/shard_map/all_gather | solution.py:213
  123.4 1.2 fusion.58
  127.3 1.5 collective-permute-start.11
  128.9 1.3 collective-permute-start.10
  130.2 1.3 collective-permute-start.9
  133.5 32.9 %shard_map.64 = (f32[128,1536]{1,0:T(8,128)}, f32[1,1536]{1,0:T(1,128)}, f32[1,1536]{1,0:T(1,128)}) custom-call(s32[36]{0:T(128)} %concatenate.38.scalars, bf16[128,1536]{1,0:T(8,128)(2,1)} %bitcast.72, s32[1,1536]{1,0:T(1,128)S(1)} %bitcast.77, s32[384,512]{1,0:T(8,128)S(1)} %broadcast_in_dim.52.kpos_ref, bf16[32,272,384]{2,1,0:T(8,128)(2,1)} %bitcast.69), custom_call_target="tpu_custom_call" | custom-call | tf_op jit(solution)/shard_map/pallas_call | solution.py:119
  166.4 4.0 %collective-permute-done.10 = f32[1,1536]{1,0:T(1,128)S(1)} collective-permute-done((f32[1,1536]{1,0:T(1,128)S(1)}, f32[1,1536]{1,0:T(1,128)S(1)}, u32[]{:S(2)}, u32[]{:S(2)}) %collective-permute-start.10) | collective-permute-done | bytes 6176 | tf_op jit(solution)/shard_map/ppermute | solution.py:258
  172.0 1.5 fusion.25
  (102 shorter events, 25.1 us)
Async XLA Ops:
  6.5 1.6 copy-start
  6.5 116.9 %all-gather.2.cloned.1.call-start = ((), (), s32[]{:S(2)}) async-start(), calls=%async_computation | async-start | bytes 6893568 | tf_op jit(solution)/shard_map/all_gather | solution.py:213
  7.4 24.8 %copy-start.14 = (pred[384]{0:T(512)(128)(4,1)}, pred[384]{0:T(512)(128)(4,1)S(1)}, u32[]{:S(2)}) copy-start(pred[384]{0:T(512)(128)(4,1)S(1)} %get-tuple-element.50) | copy-start | bytes 1156
  10.2 17.0 %collective-permute-start = (bf16[384,512]{1,0:T(8,128)(2,1)S(1)}, bf16[384,512]{1,0:T(8,128)(2,1)S(1)}, u32[]{:S(2)}, u32[]{:S(2)}) collective-permute-start(bf16[384,512]{1,0:T(8,128)(2,1)S(1)} %gather_fusion), channel_id=1, source_target_pairs={{0,1},{1,2},{2,3},{3,4},{4,5},{5,6},{6,7},{7,0},{8,9},{9,10},{10,1... | collective-permute-start | bytes 1179656 | tf_op jit(solution)/shard_map/ppermute | solution.py:176
  11.9 11.8 %collective-permute-start.1 = (bf16[384,512]{1,0:T(8,128)(2,1)S(1)}, bf16[384,512]{1,0:T(8,128)(2,1)S(1)}, u32[]{:S(2)}, u32[]{:S(2)}) collective-permute-start(bf16[384,512]{1,0:T(8,128)(2,1)S(1)} %gather_fusion), channel_id=1, source_target_pairs={{0,7},{1,0},{2,1},{3,2},{4,3},{5,4},{6,5},{7,6},{8,15},{9,8},{10,9... | collective-permute-start | bytes 1179656 | tf_op jit(solution)/shard_map/ppermute | solution.py:177
  17.2 37.2 %copy-start.16 = (f32[64]{0:T(128)}, f32[64]{0:T(128)S(1)}, u32[]{:S(2)}) copy-start(f32[64]{0:T(128)S(1)} %multiply_exponential_fusion) | copy-start | bytes 772
  17.3 22.7 %copy-start.11 = (bf16[4096,128]{1,0:T(8,128)(2,1)S(1)}, bf16[4096,128]{1,0:T(8,128)(2,1)}, u32[]{:S(2)}) copy-start(bf16[4096,128]{1,0:T(8,128)(2,1)} %param.14) | copy-start | bytes 3145732
  17.4 23.3 %copy-start.12 = (bf16[4096,128]{1,0:T(8,128)(2,1)S(1)}, bf16[4096,128]{1,0:T(8,128)(2,1)}, u32[]{:S(2)}) copy-start(bf16[4096,128]{1,0:T(8,128)(2,1)} %param.15) | copy-start | bytes 3145732
  23.7 13.5 %copy-start.7 = (bf16[384,512]{1,0:T(8,128)(2,1)}, bf16[384,512]{1,0:T(8,128)(2,1)S(1)}, u32[]{:S(2)}) copy-start(bf16[384,512]{1,0:T(8,128)(2,1)S(1)} %collective-permute-done.1) | copy-start | bytes 1179652
  23.8 13.5 %collective-permute-start.3 = (bf16[384,512]{1,0:T(8,128)(2,1)S(1)}, bf16[384,512]{1,0:T(8,128)(2,1)S(1)}, u32[]{:S(2)}, u32[]{:S(2)}) collective-permute-start(bf16[384,512]{1,0:T(8,128)(2,1)S(1)} %collective-permute-done.1), channel_id=1, source_target_pairs={{0,7},{1,0},{2,1},{3,2},{4,3},{5,4},{6,5},{7,6},{8,15},{9,8},{10,9... | collective-permute-start | bytes 1179656 | tf_op jit(solution)/shard_map/ppermute | solution.py:177
  27.2 5.0 %copy-start.6 = (bf16[384,512]{1,0:T(8,128)(2,1)}, bf16[384,512]{1,0:T(8,128)(2,1)S(1)}, u32[]{:S(2)}) copy-start(bf16[384,512]{1,0:T(8,128)(2,1)S(1)} %collective-permute-done) | copy-start | bytes 1179652
  27.2 10.1 %collective-permute-start.2 = (bf16[384,512]{1,0:T(8,128)(2,1)S(1)}, bf16[384,512]{1,0:T(8,128)(2,1)S(1)}, u32[]{:S(2)}, u32[]{:S(2)}) collective-permute-start(bf16[384,512]{1,0:T(8,128)(2,1)S(1)} %collective-permute-done), channel_id=1, source_target_pairs={{0,1},{1,2},{2,3},{3,4},{4,5},{5,6},{6,7},{7,0},{8,9},{9,10},{10,1... | collective-permute-start | bytes 1179656 | tf_op jit(solution)/shard_map/ppermute | solution.py:176
  37.2 17.2 %copy-start.8 = (bf16[384,512]{1,0:T(8,128)(2,1)}, bf16[384,512]{1,0:T(8,128)(2,1)S(1)}, u32[]{:S(2)}) copy-start(bf16[384,512]{1,0:T(8,128)(2,1)S(1)} %collective-permute-done.2) | copy-start | bytes 1179652
  37.2 9.2 %collective-permute-start.4 = (bf16[384,512]{1,0:T(8,128)(2,1)S(1)}, bf16[384,512]{1,0:T(8,128)(2,1)S(1)}, u32[]{:S(2)}, u32[]{:S(2)}) collective-permute-start(bf16[384,512]{1,0:T(8,128)(2,1)S(1)} %collective-permute-done.2), channel_id=1, source_target_pairs={{0,1},{1,2},{2,3},{3,4},{4,5},{5,6},{6,7},{7,0},{8,9},{9,10},{10,1... | collective-permute-start | bytes 1179656 | tf_op jit(solution)/shard_map/ppermute | solution.py:176
  37.3 12.9 %copy-start.4 = (bf16[384,512]{1,0:T(8,128)(2,1)}, bf16[384,512]{1,0:T(8,128)(2,1)S(1)}, u32[]{:S(2)}) copy-start(bf16[384,512]{1,0:T(8,128)(2,1)S(1)} %collective-permute-done.3) | copy-start | bytes 1179652
  37.3 9.3 %collective-permute-start.5 = (bf16[384,512]{1,0:T(8,128)(2,1)S(1)}, bf16[384,512]{1,0:T(8,128)(2,1)S(1)}, u32[]{:S(2)}, u32[]{:S(2)}) collective-permute-start(bf16[384,512]{1,0:T(8,128)(2,1)S(1)} %collective-permute-done.3), channel_id=1, source_target_pairs={{0,7},{1,0},{2,1},{3,2},{4,3},{5,4},{6,5},{7,6},{8,15},{9,8},{10,9... | collective-permute-start | bytes 1179656 | tf_op jit(solution)/shard_map/ppermute | solution.py:177
  46.5 5.8 %collective-permute-start.6 = (bf16[192,512]{1,0:T(8,128)(2,1)S(1)}, bf16[192,512]{1,0:T(8,128)(2,1)S(1)}, u32[]{:S(2)}, u32[]{:S(2)}) collective-permute-start(bf16[192,512]{1,0:T(8,128)(2,1)S(1)} %slice.44), channel_id=1, source_target_pairs={{0,1},{1,2},{2,3},{3,4},{4,5},{5,6},{6,7},{7,0},{8,9},{9,10},{10,1... | collective-permute-start | bytes 589832 | tf_op jit(solution)/shard_map/ppermute | solution.py:182
  46.6 5.7 %collective-permute-start.7 = (bf16[192,512]{1,0:T(8,128)(2,1)S(1)}, bf16[192,512]{1,0:T(8,128)(2,1)S(1)}, u32[]{:S(2)}, u32[]{:S(2)}) collective-permute-start(bf16[192,512]{1,0:T(8,128)(2,1)S(1)} %slice.45), channel_id=1, source_target_pairs={{0,7},{1,0},{2,1},{3,2},{4,3},{5,4},{6,5},{7,6},{8,15},{9,8},{10,9... | collective-permute-start | bytes 589832 | tf_op jit(solution)/shard_map/ppermute | solution.py:183
  52.3 0.7 copy-start.1
  64.0 4.4 %copy-start.3 = (bf16[4096,512]{1,0:T(8,128)(2,1)S(1)}, bf16[4096,512]{1,0:T(8,128)(2,1)}, u32[]{:S(2)}) copy-start(bf16[4096,512]{1,0:T(8,128)(2,1)} %param.13) | copy-start | bytes 12582916
  64.0 5.8 %copy-start.5 = (bf16[384,512]{1,0:T(8,128)(2,1)S(1)}, bf16[384,512]{1,0:T(8,128)(2,1)}, u32[]{:S(2)}) copy-start(bf16[384,512]{1,0:T(8,128)(2,1)} %copy-done.4) | copy-start | bytes 1179652
  65.2 5.0 %copy-start.9 = (bf16[384,512]{1,0:T(8,128)(2,1)S(1)}, bf16[384,512]{1,0:T(8,128)(2,1)}, u32[]{:S(2)}) copy-start(bf16[384,512]{1,0:T(8,128)(2,1)} %copy-done.8) | copy-start | bytes 1179652
  68.4 2.6 %copy-start.2 = (bf16[384,512]{1,0:T(8,128)(2,1)S(1)}, bf16[384,512]{1,0:T(8,128)(2,1)}, u32[]{:S(2)}) copy-start(bf16[384,512]{1,0:T(8,128)(2,1)} %copy-done.1) | copy-start | bytes 1179652
  72.6 53.5 %copy-start.13 = (s32[384]{0:T(512)S(1)}, s32[384]{0:T(512)}, u32[]{:S(2)}) copy-start(s32[384]{0:T(512)} %param.11) | copy-start | bytes 4612
  77.2 49.0 %copy-start.10 = (bf16[1536,128]{0,1:T(8,128)(2,1)}, bf16[1536,128]{0,1:T(8,128)(2,1)S(1)}, u32[]{:S(2)}) copy-start(bf16[1536,128]{0,1:T(8,128)(2,1)S(1)} %reshape.185) | copy-start | bytes 1179652
  77.2 48.8 %collective-permute-start.8 = (bf16[128,1536]{1,0:T(8,128)(2,1)S(1)}, bf16[128,1536]{1,0:T(8,128)(2,1)}, u32[]{:S(2)}, u32[]{:S(2)}) collective-permute-start(bf16[128,1536]{1,0:T(8,128)(2,1)S(1)} %bitcast.71), channel_id=1, source_target_pairs={{128,120},{136,112},{144,104},{152,96},{160,88},{168,80},{176,72},... | collective-permute-start | bytes 1179656 | tf_op jit(solution)/shard_map/ppermute | solution.py:240
  126.2 2.6 %copy-start.15 = (pred[384]{0:T(512)(128)(4,1)S(1)}, pred[384]{0:T(512)(128)(4,1)}, u32[]{:S(2)}) copy-start(pred[384]{0:T(512)(128)(4,1)} %copy-done.14) | copy-start | bytes 1156
  126.2 2.6 %copy-start.17 = (f32[384]{0:T(512)S(1)}, f32[384]{0:T(512)}, u32[]{:S(2)}) copy-start(f32[384]{0:T(512)} %param.12) | copy-start | bytes 4612
  127.3 44.6 %collective-permute-start.11 = (f32[128,1536]{1,0:T(8,128)}, f32[128,1536]{1,0:T(8,128)}, u32[]{:S(2)}, u32[]{:S(2)}) collective-permute-start(f32[128,1536]{1,0:T(8,128)} %get-tuple-element.39), channel_id=1, source_target_pairs={{0,248},{8,240},{16,232},{24,224},{32,216},{40,208},{48,200},{56,1... | collective-permute-start | bytes 2359304 | tf_op jit(solution)/shard_map/ppermute | solution.py:258
  128.9 41.6 %collective-permute-start.10 = (f32[1,1536]{1,0:T(1,128)S(1)}, f32[1,1536]{1,0:T(1,128)S(1)}, u32[]{:S(2)}, u32[]{:S(2)}) collective-permute-start(f32[1,1536]{1,0:T(1,128)S(1)} %get-tuple-element.40), channel_id=1, source_target_pairs={{0,248},{8,240},{16,232},{24,224},{32,216},{40,208},{48,200},{56,1... | collective-permute-start | bytes 18440 | tf_op jit(solution)/shard_map/ppermute | solution.py:258
  130.2 40.3 %collective-permute-start.9 = (f32[1,1536]{1,0:T(1,128)S(1)}, f32[1,1536]{1,0:T(1,128)S(1)}, u32[]{:S(2)}, u32[]{:S(2)}) collective-permute-start(f32[1,1536]{1,0:T(1,128)S(1)} %get-tuple-element.41), channel_id=1, source_target_pairs={{0,248},{8,240},{16,232},{24,224},{32,216},{40,208},{48,200},{56,1... | collective-permute-start | bytes 18440 | tf_op jit(solution)/shard_map/ppermute | solution.py:258
Sparse Core Ops, SparseCore 0:
  64.1 59.2 all-gather.1
where the time goes:
time: 184 us; the launch traced here: 182 us
  waiting for transfers between devices  60 us (33%)
  Pallas kernels  32.9 us (18%)
  starting transfers between devices  26 us (14%)
  matrix products  20.3 us (11%)
  between operations  15.5 us (8%)
  local copies, waits for them, and re-layouts  15.1 us (8%)
  other arithmetic  11.8 us (6%)
    all_gather x1, waiting for transfers between devices, body(): payload = lax.all_gather(payload, 'ctx', axis=0, tiled=True)  39.1 us
    pallas_call x1, Pallas kernels, attend(): pl.pallas_call(kernel, grid_spec=grid_spec, out_shape=[jax.ShapeDtypeStru...  32.9 us
    dot_general x24, matrix products, partial(): jnp.dot(block, lax.dynamic_slice_in_dim(w, start, width, axis=0), preferr...  20.3 us
    ppermute x3, starting transfers between devices, ring_project(): behind = lax.ppermute(behind, axis, backward)  10.2 us
    ppermute x3, waiting for transfers between devices, ring_project(): ahead = lax.ppermute(ahead, axis, forward)  9.6 us
    ppermute x1, starting transfers between devices, body(): lax.ppermute(own_q, 'ctx', [(j, shards - 1 - j) for j in range(half, shar...  7.07 us
    ppermute x3, waiting for transfers between devices, ring_project(): behind = lax.ppermute(behind, axis, backward)  5.03 us
    ppermute x3, starting transfers between devices, body(): lax.ppermute(guest_state, 'ctx', [(j, shards - 1 - j) for j in range(half)])  4.1 us
  transfers between devices with their start and end apart: 13, of which 6 were waited for; matrix products, arithmetic and copies ran while one was open for 15% of the time, Pallas kernels for 18%

commit v1 on v0

--- a/solution.py
+++ b/solution.py
@@ -14,6 +14,7 @@
 ROPE_BASE = 500000.0
 MASKED = -1e30
 SUB = 128
+STATE_ROWS = 8
 
 
 def rotate(values_in, position):
@@ -31,7 +32,7 @@
     )
 
 
-def attend_kernel(scalars, q_ref, qpos_ref, kpos_ref, kv_ref, acc_ref, m_ref, l_ref, *, cols, steps):
+def attend_kernel(scalars, q_ref, qpos_ref, kpos_ref, kv_ref, state_ref, *, cols, steps):
     i = pl.program_id(0)
     first = scalars[0]
     active = i < scalars[1]
@@ -43,11 +44,14 @@
     head_dim = q_ref.shape[0]
     pieces = kv_ref.shape[1] // SUB
 
+    acc_ref = state_ref.at[0:head_dim, :]
+    m_ref = state_ref.at[head_dim:head_dim + 1, :]
+    l_ref = state_ref.at[head_dim + 1:head_dim + 2, :]
+
     @pl.when(i == 0)
     def _():
+        state_ref[...] = jnp.zeros(state_ref.shape, jnp.float32)
         m_ref[...] = jnp.full(m_ref.shape, MASKED, jnp.float32)
-        l_ref[...] = jnp.zeros(l_ref.shape, jnp.float32)
-        acc_ref[...] = jnp.zeros(acc_ref.shape, jnp.float32)
 
     def step(qb, width, diagonal):
         c0 = qb * cols
@@ -110,28 +114,21 @@
             pl.BlockSpec((slots, cols), fixed),
             pl.BlockSpec((None, SUB + head_dim, slots), shard_of),
         ],
-        out_specs=[
-            pl.BlockSpec((head_dim, q_rows), fixed),
-            pl.BlockSpec((1, q_rows), fixed),
-            pl.BlockSpec((1, q_rows), fixed),
-        ],
+        out_specs=pl.BlockSpec((head_dim + STATE_ROWS, q_rows), fixed),
     )
     return pl.pallas_call(
         kernel,
         grid_spec=grid_spec,
-        out_shape=[
-            jax.ShapeDtypeStruct((head_dim, q_rows), jnp.float32),
-            jax.ShapeDtypeStruct((1, q_rows), jnp.float32),
-            jax.ShapeDtypeStruct((1, q_rows), jnp.float32),
-        ],
+        out_shape=jax.ShapeDtypeStruct((head_dim + STATE_ROWS, q_rows), jnp.float32),
         compiler_params=pltpu.CompilerParams(dimension_semantics=("arbitrary",)),
         interpret=interpret,
     )(scalars, q, qpos, kpos, kv)
 
 
 def merge(first, second):
-    acc_a, m_a, l_a = first
-    acc_b, m_b, l_b = second
+    head_dim = first.shape[0] - STATE_ROWS
+    acc_a, m_a, l_a = first[:head_dim], first[head_dim:head_dim + 1], first[head_dim + 1:head_dim + 2]
+    acc_b, m_b, l_b = second[:head_dim], second[head_dim:head_dim + 1], second[head_dim + 1:head_dim + 2]
     m_a = jnp.where(l_a > 0.0, m_a, MASKED)
     m_b = jnp.where(l_b > 0.0, m_b, MASKED)
     m = jnp.maximum(m_a, m_b)
@@ -141,7 +138,7 @@
 
 
 FLAG_ROWS = 16
-EXTRA_OWN = 1
+EXTRA_OWN = 4
 
 
 def pack_payload(key_rows, value_rows, live):
@@ -244,15 +241,10 @@
     )
 
     def guest_work(q):
-        return tuple(attend(guest_scalars, q, query_pos, own_pos, blocks, half - EXTRA_OWN))
+        return attend(guest_scalars, q, query_pos, own_pos, blocks, half - EXTRA_OWN)
 
     def no_guest(q):
-        rows = (1, q.shape[1])
-        return (
-            jnp.zeros(q.shape, jnp.float32),
-            jnp.full(rows, MASKED, jnp.float32),
-            jnp.zeros(rows, jnp.float32),
-        )
+        return jnp.zeros((q.shape[0] + STATE_ROWS, q.shape[1]), jnp.float32)
 
     guest_state = lax.cond(guest_count > 0, guest_work, no_guest, guest_q)
     returned = lax.ppermute(guest_state, "ctx", [(j, shards - 1 - j) for j in range(half)])
@@ -261,7 +253,7 @@
     own_scalars = scalars_of(
         own_first, own - own_first + 1, live_blocks(jnp.sum(live.astype(jnp.int32))), own
     )
-    own_state = tuple(attend(own_scalars, own_q, query_pos, own_pos, blocks, half + EXTRA_OWN))
+    own_state = attend(own_scalars, own_q, query_pos, own_pos, blocks, half + EXTRA_OWN)
     acc, total = merge(own_state, returned)
     out = (acc / jnp.where(total > 0.0, total, 1.0)) * per_column(gated)
     out = jnp.transpose(out.astype(jnp.bfloat16))

time: 184 us -> 182 us (0.989)
  Pallas kernels: 32.9 us -> 39.6 us
  waiting for transfers between devices: 60 us -> 56 us
  starting transfers between devices: 26 us -> 23.5 us
    pallas_call x1, Pallas kernels: 32.9 us -> 39.6 us  [attend(): pl.pallas_call(kernel, grid_spec=grid_spec, out_shape=jax.ShapeDtypeStruc...]
    ppermute x3 -> x1, waiting for transfers between devices: 4.05 us -> 0.01 us  [body(): lax.ppermute(guest_state, 'ctx', [(j, shards - 1 - j) for j in range(half)])]
    ppermute x3 -> x1, starting transfers between devices: 4.1 us -> 1.5 us  [body(): lax.ppermute(guest_state, 'ctx', [(j, shards - 1 - j) for j in range(half)])]
  transfers between devices with their start and end apart: 13 -> 11, of which waited for: 6 -> 5; matrix products, arithmetic and copies ran while one was open for 15% -> 15% of each run, Pallas kernels for 18% -> 22%
where the time goes in v1:
time: 182 us; the launch traced here: 181 us
  waiting for transfers between devices  56 us (31%)
  Pallas kernels  39.6 us (22%)
  starting transfers between devices  23.5 us (13%)
  matrix products  20.2 us (11%)
  between operations  15.6 us (9%)
  local copies, waits for them, and re-layouts  15.1 us (8%)
  other arithmetic  11.3 us (6%)
    pallas_call x1, Pallas kernels, attend(): pl.pallas_call(kernel, grid_spec=grid_spec, out_shape=jax.ShapeDtypeStruc...  39.6 us
    all_gather x1, waiting for transfers between devices, body(): payload = lax.all_gather(payload, 'ctx', axis=0, tiled=True)  39.1 us
    dot_general x24, matrix products, partial(): jnp.dot(block, lax.dynamic_slice_in_dim(w, start, width, axis=0), preferr...  20.2 us
    ppermute x3, starting transfers between devices, ring_project(): behind = lax.ppermute(behind, axis, backward)  10.2 us
    ppermute x3, waiting for transfers between devices, ring_project(): ahead = lax.ppermute(ahead, axis, forward)  9.61 us
    ppermute x1, starting transfers between devices, body(): lax.ppermute(own_q, 'ctx', [(j, shards - 1 - j) for j in range(half, shar...  7.08 us
    ppermute x3, waiting for transfers between devices, ring_project(): behind = lax.ppermute(behind, axis, backward)  5.03 us
  transfers between devices with their start and end apart: 11, of which 5 were waited for; matrix products, arithmetic and copies ran while one was open for 15% of the time, Pallas kernels for 22%

profile of v1, /device:TPU:31, one launch (start us, length us, event | category | flops | bytes accessed | tf_op | source)
XLA Modules:
  0.0 181.2 jit_solution(5476658269418182276)
XLA Ops:
  8.1 2.1 %gather_fusion = bf16[384,512]{1,0:T(8,128)(2,1)S(1)} fusion(bf16[2048,512]{1,0:T(8,128)(2,1)S(1)} %copy-done, s32[1024]{0:T(1024)S(1)} %pad_clamp_fusion), kind=kCustom, calls=%fused_computation | custom fusion | bytes 787968 | tf_op jit(solution)/shard_map/gather | solution.py:199
  10.2 1.7 collective-permute-start
  11.9 4.0 %collective-permute-start.1 = (bf16[384,512]{1,0:T(8,128)(2,1)S(1)}, bf16[384,512]{1,0:T(8,128)(2,1)S(1)}, u32[]{:S(2)}, u32[]{:S(2)}) collective-permute-start(bf16[384,512]{1,0:T(8,128)(2,1)S(1)} %gather_fusion), channel_id=1, source_target_pairs={{0,7},{1,0},{2,1},{3,2},{4,3},{5,4},{6,5},{7,6},{8,15},{9,8},{10,9... | collective-permute-start | bytes 1179656 | tf_op jit(solution)/shard_map/ppermute | solution.py:174
  15.9 1.2 fusion.56
  17.4 1.3 fusion.44
  18.7 5.0 %collective-permute-done.1 = bf16[384,512]{1,0:T(8,128)(2,1)S(1)} collective-permute-done((bf16[384,512]{1,0:T(8,128)(2,1)S(1)}, bf16[384,512]{1,0:T(8,128)(2,1)S(1)}, u32[]{:S(2)}, u32[]{:S(2)}) %collective-permute-start.1) | collective-permute-done | bytes 393248 | tf_op jit(solution)/shard_map/ppermute | solution.py:174
  23.8 3.4 %collective-permute-start.3 = (bf16[384,512]{1,0:T(8,128)(2,1)S(1)}, bf16[384,512]{1,0:T(8,128)(2,1)S(1)}, u32[]{:S(2)}, u32[]{:S(2)}) collective-permute-start(bf16[384,512]{1,0:T(8,128)(2,1)S(1)} %collective-permute-done.1), channel_id=1, source_target_pairs={{0,7},{1,0},{2,1},{3,2},{4,3},{5,4},{6,5},{7,6},{8,15},{9,8},{10,9... | collective-permute-start | bytes 1179656 | tf_op jit(solution)/shard_map/ppermute | solution.py:174
  27.2 1.4 convolution_add_fusion.11
  28.5 1.2 convolution_add_fusion.7
  29.7 1.2 convolution_add_fusion.10
  31.0 1.2 convolution_add_fusion.6
  32.2 5.0 %collective-permute-done.2 = bf16[384,512]{1,0:T(8,128)(2,1)S(1)} collective-permute-done((bf16[384,512]{1,0:T(8,128)(2,1)S(1)}, bf16[384,512]{1,0:T(8,128)(2,1)S(1)}, u32[]{:S(2)}, u32[]{:S(2)}) %collective-permute-start.2) | collective-permute-done | bytes 393248 | tf_op jit(solution)/shard_map/ppermute | solution.py:173
  37.3 2.7 %collective-permute-start.5 = (bf16[384,512]{1,0:T(8,128)(2,1)S(1)}, bf16[384,512]{1,0:T(8,128)(2,1)S(1)}, u32[]{:S(2)}, u32[]{:S(2)}) collective-permute-start(bf16[384,512]{1,0:T(8,128)(2,1)S(1)} %collective-permute-done.3), channel_id=1, source_target_pairs={{0,7},{1,0},{2,1},{3,2},{4,3},{5,4},{6,5},{7,6},{8,15},{9,8},{10,9... | collective-permute-start | bytes 1179656 | tf_op jit(solution)/shard_map/ppermute | solution.py:174
  41.9 4.6 %collective-permute-done.4 = bf16[384,512]{1,0:T(8,128)(2,1)S(1)} collective-permute-done((bf16[384,512]{1,0:T(8,128)(2,1)S(1)}, bf16[384,512]{1,0:T(8,128)(2,1)S(1)}, u32[]{:S(2)}, u32[]{:S(2)}) %collective-permute-start.4) | collective-permute-done | bytes 393248 | tf_op jit(solution)/shard_map/ppermute | solution.py:173
  46.6 2.9 %collective-permute-start.7 = (bf16[192,512]{1,0:T(8,128)(2,1)S(1)}, bf16[192,512]{1,0:T(8,128)(2,1)S(1)}, u32[]{:S(2)}, u32[]{:S(2)}) collective-permute-start(bf16[192,512]{1,0:T(8,128)(2,1)S(1)} %slice.69), channel_id=1, source_target_pairs={{0,7},{1,0},{2,1},{3,2},{4,3},{5,4},{6,5},{7,6},{8,15},{9,8},{10,9... | collective-permute-start | bytes 589832 | tf_op jit(solution)/shard_map/ppermute | solution.py:180
  50.1 2.2 %collective-permute-done.6 = bf16[192,512]{1,0:T(8,128)(2,1)S(1)} collective-permute-done((bf16[192,512]{1,0:T(8,128)(2,1)S(1)}, bf16[192,512]{1,0:T(8,128)(2,1)S(1)}, u32[]{:S(2)}, u32[]{:S(2)}) %collective-permute-start.6) | collective-permute-done | bytes 196640 | tf_op jit(solution)/shard_map/ppermute | solution.py:179
  56.3 1.4 concatenate.35
  59.3 1.6 copy.10
  60.9 1.4 fusion.10
  62.3 1.6 pad_maximum_fusion
  64.0 1.2 multiply_cosine_fusion
  65.2 1.6 fusion.27
  66.8 1.5 convolution_add_fusion.3
  68.3 1.4 convolution_add_fusion.2
  71.3 1.3 fusion.2
  72.6 1.4 copy.15
  77.2 7.1 %collective-permute-start.8 = (bf16[128,1536]{1,0:T(8,128)(2,1)S(1)}, bf16[128,1536]{1,0:T(8,128)(2,1)}, u32[]{:S(2)}, u32[]{:S(2)}) collective-permute-start(bf16[128,1536]{1,0:T(8,128)(2,1)S(1)} %bitcast.71), channel_id=1, source_target_pairs={{128,120},{136,112},{144,104},{152,96},{160,88},{168,80},{176,72},... | collective-permute-start | bytes 1179656 | tf_op jit(solution)/shard_map/ppermute | solution.py:237
  84.3 39.1 %all-gather.2.cloned.1.call-done = bf16[8704,384]{1,0:T(8,128)(2,1)} async-done(((bf16[272,384]{1,0:T(8,128)(2,1)}), bf16[8704,384]{1,0:T(8,128)(2,1)}) %all-gather.2.cloned.1.call-update) | async-done | bytes 6684688 | tf_op jit(solution)/shard_map/all_gather | solution.py:210
  123.4 1.2 fusion.62
  127.4 1.5 collective-permute-start.9
  131.0 39.6 %shard_map.64 = f32[136,1536]{1,0:T(8,128)} custom-call(s32[36]{0:T(128)} %concatenate.38.scalars, bf16[128,1536]{1,0:T(8,128)(2,1)} %bitcast.72, s32[1,1536]{1,0:T(1,128)S(1)} %bitcast.77, s32[384,512]{1,0:T(8,128)S(1)} %broadcast_in_dim.52.kpos_ref, bf16[32,272,384]{2,1,0:T(8,128)(2,1)} %bitcast.69), custom_call_target="tpu_custom_call" | custom-call | tf_op jit(solution)/shard_map/pallas_call | solution.py:119
  171.5 1.5 fusion.29
  (95 shorter events, 21.0 us)
Async XLA Ops:
  6.5 1.6 copy-start
  6.5 116.9 %all-gather.2.cloned.1.call-start = ((), (), s32[]{:S(2)}) async-start(), calls=%async_computation | async-start | bytes 6893568 | tf_op jit(solution)/shard_map/all_gather | solution.py:210
  7.4 24.8 %copy-start.14 = (pred[384]{0:T(512)(128)(4,1)}, pred[384]{0:T(512)(128)(4,1)S(1)}, u32[]{:S(2)}) copy-start(pred[384]{0:T(512)(128)(4,1)S(1)} %get-tuple-element.41) | copy-start | bytes 1156
  10.2 17.0 %collective-permute-start = (bf16[384,512]{1,0:T(8,128)(2,1)S(1)}, bf16[384,512]{1,0:T(8,128)(2,1)S(1)}, u32[]{:S(2)}, u32[]{:S(2)}) collective-permute-start(bf16[384,512]{1,0:T(8,128)(2,1)S(1)} %gather_fusion), channel_id=1, source_target_pairs={{0,1},{1,2},{2,3},{3,4},{4,5},{5,6},{6,7},{7,0},{8,9},{9,10},{10,1... | collective-permute-start | bytes 1179656 | tf_op jit(solution)/shard_map/ppermute | solution.py:173
  11.9 11.8 %collective-permute-start.1 = (bf16[384,512]{1,0:T(8,128)(2,1)S(1)}, bf16[384,512]{1,0:T(8,128)(2,1)S(1)}, u32[]{:S(2)}, u32[]{:S(2)}) collective-permute-start(bf16[384,512]{1,0:T(8,128)(2,1)S(1)} %gather_fusion), channel_id=1, source_target_pairs={{0,7},{1,0},{2,1},{3,2},{4,3},{5,4},{6,5},{7,6},{8,15},{9,8},{10,9... | collective-permute-start | bytes 1179656 | tf_op jit(solution)/shard_map/ppermute | solution.py:174
  17.2 37.2 %copy-start.16 = (f32[64]{0:T(128)}, f32[64]{0:T(128)S(1)}, u32[]{:S(2)}) copy-start(f32[64]{0:T(128)S(1)} %multiply_exponential_fusion) | copy-start | bytes 772
  17.3 22.7 %copy-start.11 = (bf16[4096,128]{1,0:T(8,128)(2,1)S(1)}, bf16[4096,128]{1,0:T(8,128)(2,1)}, u32[]{:S(2)}) copy-start(bf16[4096,128]{1,0:T(8,128)(2,1)} %param.14) | copy-start | bytes 3145732
  17.4 23.3 %copy-start.12 = (bf16[4096,128]{1,0:T(8,128)(2,1)S(1)}, bf16[4096,128]{1,0:T(8,128)(2,1)}, u32[]{:S(2)}) copy-start(bf16[4096,128]{1,0:T(8,128)(2,1)} %param.15) | copy-start | bytes 3145732
  23.7 13.5 %copy-start.7 = (bf16[384,512]{1,0:T(8,128)(2,1)}, bf16[384,512]{1,0:T(8,128)(2,1)S(1)}, u32[]{:S(2)}) copy-start(bf16[384,512]{1,0:T(8,128)(2,1)S(1)} %collective-permute-done.1) | copy-start | bytes 1179652
  23.8 13.5 %collective-permute-start.3 = (bf16[384,512]{1,0:T(8,128)(2,1)S(1)}, bf16[384,512]{1,0:T(8,128)(2,1)S(1)}, u32[]{:S(2)}, u32[]{:S(2)}) collective-permute-start(bf16[384,512]{1,0:T(8,128)(2,1)S(1)} %collective-permute-done.1), channel_id=1, source_target_pairs={{0,7},{1,0},{2,1},{3,2},{4,3},{5,4},{6,5},{7,6},{8,15},{9,8},{10,9... | collective-permute-start | bytes 1179656 | tf_op jit(solution)/shard_map/ppermute | solution.py:174
  27.2 5.0 %copy-start.6 = (bf16[384,512]{1,0:T(8,128)(2,1)}, bf16[384,512]{1,0:T(8,128)(2,1)S(1)}, u32[]{:S(2)}) copy-start(bf16[384,512]{1,0:T(8,128)(2,1)S(1)} %collective-permute-done) | copy-start | bytes 1179652
  27.2 10.1 %collective-permute-start.2 = (bf16[384,512]{1,0:T(8,128)(2,1)S(1)}, bf16[384,512]{1,0:T(8,128)(2,1)S(1)}, u32[]{:S(2)}, u32[]{:S(2)}) collective-permute-start(bf16[384,512]{1,0:T(8,128)(2,1)S(1)} %collective-permute-done), channel_id=1, source_target_pairs={{0,1},{1,2},{2,3},{3,4},{4,5},{5,6},{6,7},{7,0},{8,9},{9,10},{10,1... | collective-permute-start | bytes 1179656 | tf_op jit(solution)/shard_map/ppermute | solution.py:173
  37.2 17.1 %copy-start.8 = (bf16[384,512]{1,0:T(8,128)(2,1)}, bf16[384,512]{1,0:T(8,128)(2,1)S(1)}, u32[]{:S(2)}) copy-start(bf16[384,512]{1,0:T(8,128)(2,1)S(1)} %collective-permute-done.2) | copy-start | bytes 1179652
  37.2 9.2 %collective-permute-start.4 = (bf16[384,512]{1,0:T(8,128)(2,1)S(1)}, bf16[384,512]{1,0:T(8,128)(2,1)S(1)}, u32[]{:S(2)}, u32[]{:S(2)}) collective-permute-start(bf16[384,512]{1,0:T(8,128)(2,1)S(1)} %collective-permute-done.2), channel_id=1, source_target_pairs={{0,1},{1,2},{2,3},{3,4},{4,5},{5,6},{6,7},{7,0},{8,9},{9,10},{10,1... | collective-permute-start | bytes 1179656 | tf_op jit(solution)/shard_map/ppermute | solution.py:173
  37.3 12.9 %copy-start.4 = (bf16[384,512]{1,0:T(8,128)(2,1)}, bf16[384,512]{1,0:T(8,128)(2,1)S(1)}, u32[]{:S(2)}) copy-start(bf16[384,512]{1,0:T(8,128)(2,1)S(1)} %collective-permute-done.3) | copy-start | bytes 1179652
  37.3 9.3 %collective-permute-start.5 = (bf16[384,512]{1,0:T(8,128)(2,1)S(1)}, bf16[384,512]{1,0:T(8,128)(2,1)S(1)}, u32[]{:S(2)}, u32[]{:S(2)}) collective-permute-start(bf16[384,512]{1,0:T(8,128)(2,1)S(1)} %collective-permute-done.3), channel_id=1, source_target_pairs={{0,7},{1,0},{2,1},{3,2},{4,3},{5,4},{6,5},{7,6},{8,15},{9,8},{10,9... | collective-permute-start | bytes 1179656 | tf_op jit(solution)/shard_map/ppermute | solution.py:174
  46.5 5.8 %collective-permute-start.6 = (bf16[192,512]{1,0:T(8,128)(2,1)S(1)}, bf16[192,512]{1,0:T(8,128)(2,1)S(1)}, u32[]{:S(2)}, u32[]{:S(2)}) collective-permute-start(bf16[192,512]{1,0:T(8,128)(2,1)S(1)} %slice.68), channel_id=1, source_target_pairs={{0,1},{1,2},{2,3},{3,4},{4,5},{5,6},{6,7},{7,0},{8,9},{9,10},{10,1... | collective-permute-start | bytes 589832 | tf_op jit(solution)/shard_map/ppermute | solution.py:179
  46.6 5.7 %collective-permute-start.7 = (bf16[192,512]{1,0:T(8,128)(2,1)S(1)}, bf16[192,512]{1,0:T(8,128)(2,1)S(1)}, u32[]{:S(2)}, u32[]{:S(2)}) collective-permute-start(bf16[192,512]{1,0:T(8,128)(2,1)S(1)} %slice.69), channel_id=1, source_target_pairs={{0,7},{1,0},{2,1},{3,2},{4,3},{5,4},{6,5},{7,6},{8,15},{9,8},{10,9... | collective-permute-start | bytes 589832 | tf_op jit(solution)/shard_map/ppermute | solution.py:180
  52.3 0.7 copy-start.1
  64.0 4.4 %copy-start.3 = (bf16[4096,512]{1,0:T(8,128)(2,1)S(1)}, bf16[4096,512]{1,0:T(8,128)(2,1)}, u32[]{:S(2)}) copy-start(bf16[4096,512]{1,0:T(8,128)(2,1)} %param.13) | copy-start | bytes 12582916
  64.0 5.8 %copy-start.5 = (bf16[384,512]{1,0:T(8,128)(2,1)S(1)}, bf16[384,512]{1,0:T(8,128)(2,1)}, u32[]{:S(2)}) copy-start(bf16[384,512]{1,0:T(8,128)(2,1)} %copy-done.4) | copy-start | bytes 1179652
  65.2 5.0 %copy-start.9 = (bf16[384,512]{1,0:T(8,128)(2,1)S(1)}, bf16[384,512]{1,0:T(8,128)(2,1)}, u32[]{:S(2)}) copy-start(bf16[384,512]{1,0:T(8,128)(2,1)} %copy-done.8) | copy-start | bytes 1179652
  68.3 2.6 %copy-start.2 = (bf16[384,512]{1,0:T(8,128)(2,1)S(1)}, bf16[384,512]{1,0:T(8,128)(2,1)}, u32[]{:S(2)}) copy-start(bf16[384,512]{1,0:T(8,128)(2,1)} %copy-done.1) | copy-start | bytes 1179652
  72.6 53.6 %copy-start.13 = (s32[384]{0:T(512)S(1)}, s32[384]{0:T(512)}, u32[]{:S(2)}) copy-start(s32[384]{0:T(512)} %param.11) | copy-start | bytes 4612
  77.2 49.1 %copy-start.10 = (bf16[1536,128]{0,1:T(8,128)(2,1)}, bf16[1536,128]{0,1:T(8,128)(2,1)S(1)}, u32[]{:S(2)}) copy-start(bf16[1536,128]{0,1:T(8,128)(2,1)S(1)} %reshape.185) | copy-start | bytes 1179652
  77.2 48.9 %collective-permute-start.8 = (bf16[128,1536]{1,0:T(8,128)(2,1)S(1)}, bf16[128,1536]{1,0:T(8,128)(2,1)}, u32[]{:S(2)}, u32[]{:S(2)}) collective-permute-start(bf16[128,1536]{1,0:T(8,128)(2,1)S(1)} %bitcast.71), channel_id=1, source_target_pairs={{128,120},{136,112},{144,104},{152,96},{160,88},{168,80},{176,72},... | collective-permute-start | bytes 1179656 | tf_op jit(solution)/shard_map/ppermute | solution.py:237
  126.3 2.6 %copy-start.15 = (pred[384]{0:T(512)(128)(4,1)S(1)}, pred[384]{0:T(512)(128)(4,1)}, u32[]{:S(2)}) copy-start(pred[384]{0:T(512)(128)(4,1)} %copy-done.14) | copy-start | bytes 1156
  126.3 4.1 %copy-start.17 = (f32[384]{0:T(512)S(1)}, f32[384]{0:T(512)}, u32[]{:S(2)}) copy-start(f32[384]{0:T(512)} %param.12) | copy-start | bytes 4612
  127.4 43.2 %collective-permute-start.9 = (f32[136,1536]{1,0:T(8,128)}, f32[136,1536]{1,0:T(8,128)}, u32[]{:S(2)}, u32[]{:S(2)}) collective-permute-start(f32[136,1536]{1,0:T(8,128)} %get-tuple-element.49), channel_id=1, source_target_pairs={{0,248},{8,240},{16,232},{24,224},{32,216},{40,208},{48,200},{56,1... | collective-permute-start | bytes 2506760 | tf_op jit(solution)/shard_map/ppermute | solution.py:250
Sparse Core Ops, SparseCore 0:
  64.1 59.2 all-gather.1

commit v2 on v1

--- a/solution.py
+++ b/solution.py
@@ -138,7 +138,7 @@
 
 
 FLAG_ROWS = 16
-EXTRA_OWN = 4
+EXTRA_OWN = 2
 
 
 def pack_payload(key_rows, value_rows, live):

time: 182 us -> 181 us (level)
  the two profiles are of different devices: /device:TPU:31 before, /device:TPU:27 now
where the time goes in v2:
time: 181 us; the launch traced here: 178 us
  waiting for transfers between devices  61.8 us (34%)
  Pallas kernels  32.6 us (18%)
  starting transfers between devices  21.8 us (12%)
  matrix products  20.2 us (11%)
  between operations  15.6 us (9%)
  local copies, waits for them, and re-layouts  15.1 us (8%)
  other arithmetic  11.3 us (6%)
    all_gather x1, waiting for transfers between devices, body(): payload = lax.all_gather(payload, 'ctx', axis=0, tiled=True)  45 us
    pallas_call x1, Pallas kernels, attend(): pl.pallas_call(kernel, grid_spec=grid_spec, out_shape=jax.ShapeDtypeStruc...  32.6 us
    dot_general x24, matrix products, partial(): jnp.dot(block, lax.dynamic_slice_in_dim(w, start, width, axis=0), preferr...  20.2 us
    ppermute x3, starting transfers between devices, ring_project(): behind = lax.ppermute(behind, axis, backward)  10.2 us
    ppermute x3, waiting for transfers between devices, ring_project(): ahead = lax.ppermute(ahead, axis, forward)  9.61 us
    ppermute x1, starting transfers between devices, body(): lax.ppermute(guest_state, 'ctx', [(j, shards - 1 - j) for j in range(half)])  5.59 us
    ppermute x3, waiting for transfers between devices, ring_project(): behind = lax.ppermute(behind, axis, backward)  5.02 us
  transfers between devices with their start and end apart: 11, of which 5 were waited for; matrix products, arithmetic and copies ran while one was open for 15% of the time, Pallas kernels for 18%

profile of v2, /device:TPU:27, one launch (start us, length us, event | category | flops | bytes accessed | tf_op | source)
XLA Modules:
  0.0 178.3 jit_solution(3092352319674694405)
XLA Ops:
  8.1 2.1 %gather_fusion = bf16[384,512]{1,0:T(8,128)(2,1)S(1)} fusion(bf16[2048,512]{1,0:T(8,128)(2,1)S(1)} %copy-done, s32[1024]{0:T(1024)S(1)} %pad_clamp_fusion), kind=kCustom, calls=%fused_computation | custom fusion | bytes 787968 | tf_op jit(solution)/shard_map/gather | solution.py:199
  10.2 1.7 collective-permute-start
  11.9 4.0 %collective-permute-start.1 = (bf16[384,512]{1,0:T(8,128)(2,1)S(1)}, bf16[384,512]{1,0:T(8,128)(2,1)S(1)}, u32[]{:S(2)}, u32[]{:S(2)}) collective-permute-start(bf16[384,512]{1,0:T(8,128)(2,1)S(1)} %gather_fusion), channel_id=1, source_target_pairs={{0,7},{1,0},{2,1},{3,2},{4,3},{5,4},{6,5},{7,6},{8,15},{9,8},{10,9... | collective-permute-start | bytes 1179656 | tf_op jit(solution)/shard_map/ppermute | solution.py:174
  15.9 1.2 fusion.56
  17.4 1.3 fusion.44
  18.7 5.0 %collective-permute-done.1 = bf16[384,512]{1,0:T(8,128)(2,1)S(1)} collective-permute-done((bf16[384,512]{1,0:T(8,128)(2,1)S(1)}, bf16[384,512]{1,0:T(8,128)(2,1)S(1)}, u32[]{:S(2)}, u32[]{:S(2)}) %collective-permute-start.1) | collective-permute-done | bytes 393248 | tf_op jit(solution)/shard_map/ppermute | solution.py:174
  23.8 3.4 %collective-permute-start.3 = (bf16[384,512]{1,0:T(8,128)(2,1)S(1)}, bf16[384,512]{1,0:T(8,128)(2,1)S(1)}, u32[]{:S(2)}, u32[]{:S(2)}) collective-permute-start(bf16[384,512]{1,0:T(8,128)(2,1)S(1)} %collective-permute-done.1), channel_id=1, source_target_pairs={{0,7},{1,0},{2,1},{3,2},{4,3},{5,4},{6,5},{7,6},{8,15},{9,8},{10,9... | collective-permute-start | bytes 1179656 | tf_op jit(solution)/shard_map/ppermute | solution.py:174
  27.2 1.4 convolution_add_fusion.11
  28.5 1.2 convolution_add_fusion.7
  29.7 1.2 convolution_add_fusion.10
  31.0 1.2 convolution_add_fusion.6
  32.2 5.1 %collective-permute-done.2 = bf16[384,512]{1,0:T(8,128)(2,1)S(1)} collective-permute-done((bf16[384,512]{1,0:T(8,128)(2,1)S(1)}, bf16[384,512]{1,0:T(8,128)(2,1)S(1)}, u32[]{:S(2)}, u32[]{:S(2)}) %collective-permute-start.2) | collective-permute-done | bytes 393248 | tf_op jit(solution)/shard_map/ppermute | solution.py:173
  37.3 2.7 %collective-permute-start.5 = (bf16[384,512]{1,0:T(8,128)(2,1)S(1)}, bf16[384,512]{1,0:T(8,128)(2,1)S(1)}, u32[]{:S(2)}, u32[]{:S(2)}) collective-permute-start(bf16[384,512]{1,0:T(8,128)(2,1)S(1)} %collective-permute-done.3), channel_id=1, source_target_pairs={{0,7},{1,0},{2,1},{3,2},{4,3},{5,4},{6,5},{7,6},{8,15},{9,8},{10,9... | collective-permute-start | bytes 1179656 | tf_op jit(solution)/shard_map/ppermute | solution.py:174
  41.9 4.5 %collective-permute-done.4 = bf16[384,512]{1,0:T(8,128)(2,1)S(1)} collective-permute-done((bf16[384,512]{1,0:T(8,128)(2,1)S(1)}, bf16[384,512]{1,0:T(8,128)(2,1)S(1)}, u32[]{:S(2)}, u32[]{:S(2)}) %collective-permute-start.4) | collective-permute-done | bytes 393248 | tf_op jit(solution)/shard_map/ppermute | solution.py:173
  46.6 2.9 %collective-permute-start.7 = (bf16[192,512]{1,0:T(8,128)(2,1)S(1)}, bf16[192,512]{1,0:T(8,128)(2,1)S(1)}, u32[]{:S(2)}, u32[]{:S(2)}) collective-permute-start(bf16[192,512]{1,0:T(8,128)(2,1)S(1)} %slice.69), channel_id=1, source_target_pairs={{0,7},{1,0},{2,1},{3,2},{4,3},{5,4},{6,5},{7,6},{8,15},{9,8},{10,9... | collective-permute-start | bytes 589832 | tf_op jit(solution)/shard_map/ppermute | solution.py:180
  50.1 2.2 %collective-permute-done.6 = bf16[192,512]{1,0:T(8,128)(2,1)S(1)} collective-permute-done((bf16[192,512]{1,0:T(8,128)(2,1)S(1)}, bf16[192,512]{1,0:T(8,128)(2,1)S(1)}, u32[]{:S(2)}, u32[]{:S(2)}) %collective-permute-start.6) | collective-permute-done | bytes 196640 | tf_op jit(solution)/shard_map/ppermute | solution.py:179
  56.3 1.4 concatenate.35
  59.3 1.6 copy.10
  60.9 1.4 fusion.10
  62.3 1.6 pad_maximum_fusion
  64.0 1.2 multiply_cosine_fusion
  65.2 1.6 fusion.27
  66.8 1.5 convolution_add_fusion.3
  68.4 1.4 convolution_add_fusion.2
  71.3 1.3 fusion.2
  72.6 1.4 copy.15
  77.2 1.3 collective-permute-start.8
  78.5 45.0 %all-gather.2.cloned.1.call-done = bf16[8704,384]{1,0:T(8,128)(2,1)} async-done(((bf16[272,384]{1,0:T(8,128)(2,1)}), bf16[8704,384]{1,0:T(8,128)(2,1)}) %all-gather.2.cloned.1.call-update) | async-done | bytes 6684688 | tf_op jit(solution)/shard_map/all_gather | solution.py:210
  123.4 1.2 fusion.62
  127.4 5.6 %collective-permute-start.9 = (f32[136,1536]{1,0:T(8,128)}, f32[136,1536]{1,0:T(8,128)}, u32[]{:S(2)}, u32[]{:S(2)}) collective-permute-start(f32[136,1536]{1,0:T(8,128)} %get-tuple-element.49), channel_id=1, source_target_pairs={{0,248},{8,240},{16,232},{24,224},{32,216},{40,208},{48,200},{56,1... | collective-permute-start | bytes 2506760 | tf_op jit(solution)/shard_map/ppermute | solution.py:250
  135.1 32.6 %shard_map.64 = f32[136,1536]{1,0:T(8,128)} custom-call(s32[36]{0:T(128)} %concatenate.38.scalars, bf16[128,1536]{1,0:T(8,128)(2,1)} %bitcast.72, s32[1,1536]{1,0:T(1,128)S(1)} %bitcast.77, s32[384,512]{1,0:T(8,128)S(1)} %broadcast_in_dim.52.kpos_ref, bf16[32,272,384]{2,1,0:T(8,128)(2,1)} %bitcast.69), custom_call_target="tpu_custom_call" | custom-call | tf_op jit(solution)/shard_map/pallas_call | solution.py:119
  168.7 1.5 fusion.29
  (95 shorter events, 21.0 us)
Async XLA Ops:
  6.5 1.6 copy-start
  6.5 116.9 %all-gather.2.cloned.1.call-start = ((), (), s32[]{:S(2)}) async-start(), calls=%async_computation | async-start | bytes 6893568 | tf_op jit(solution)/shard_map/all_gather | solution.py:210
  7.4 24.8 %copy-start.14 = (pred[384]{0:T(512)(128)(4,1)}, pred[384]{0:T(512)(128)(4,1)S(1)}, u32[]{:S(2)}) copy-start(pred[384]{0:T(512)(128)(4,1)S(1)} %get-tuple-element.41) | copy-start | bytes 1156
  10.2 17.0 %collective-permute-start = (bf16[384,512]{1,0:T(8,128)(2,1)S(1)}, bf16[384,512]{1,0:T(8,128)(2,1)S(1)}, u32[]{:S(2)}, u32[]{:S(2)}) collective-permute-start(bf16[384,512]{1,0:T(8,128)(2,1)S(1)} %gather_fusion), channel_id=1, source_target_pairs={{0,1},{1,2},{2,3},{3,4},{4,5},{5,6},{6,7},{7,0},{8,9},{9,10},{10,1... | collective-permute-start | bytes 1179656 | tf_op jit(solution)/shard_map/ppermute | solution.py:173
  11.9 11.8 %collective-permute-start.1 = (bf16[384,512]{1,0:T(8,128)(2,1)S(1)}, bf16[384,512]{1,0:T(8,128)(2,1)S(1)}, u32[]{:S(2)}, u32[]{:S(2)}) collective-permute-start(bf16[384,512]{1,0:T(8,128)(2,1)S(1)} %gather_fusion), channel_id=1, source_target_pairs={{0,7},{1,0},{2,1},{3,2},{4,3},{5,4},{6,5},{7,6},{8,15},{9,8},{10,9... | collective-permute-start | bytes 1179656 | tf_op jit(solution)/shard_map/ppermute | solution.py:174
  17.2 37.2 %copy-start.16 = (f32[64]{0:T(128)}, f32[64]{0:T(128)S(1)}, u32[]{:S(2)}) copy-start(f32[64]{0:T(128)S(1)} %multiply_exponential_fusion) | copy-start | bytes 772
  17.3 22.7 %copy-start.11 = (bf16[4096,128]{1,0:T(8,128)(2,1)S(1)}, bf16[4096,128]{1,0:T(8,128)(2,1)}, u32[]{:S(2)}) copy-start(bf16[4096,128]{1,0:T(8,128)(2,1)} %param.14) | copy-start | bytes 3145732
  17.4 23.3 %copy-start.12 = (bf16[4096,128]{1,0:T(8,128)(2,1)S(1)}, bf16[4096,128]{1,0:T(8,128)(2,1)}, u32[]{:S(2)}) copy-start(bf16[4096,128]{1,0:T(8,128)(2,1)} %param.15) | copy-start | bytes 3145732
  23.7 13.5 %copy-start.7 = (bf16[384,512]{1,0:T(8,128)(2,1)}, bf16[384,512]{1,0:T(8,128)(2,1)S(1)}, u32[]{:S(2)}) copy-start(bf16[384,512]{1,0:T(8,128)(2,1)S(1)} %collective-permute-done.1) | copy-start | bytes 1179652
  23.8 13.5 %collective-permute-start.3 = (bf16[384,512]{1,0:T(8,128)(2,1)S(1)}, bf16[384,512]{1,0:T(8,128)(2,1)S(1)}, u32[]{:S(2)}, u32[]{:S(2)}) collective-permute-start(bf16[384,512]{1,0:T(8,128)(2,1)S(1)} %collective-permute-done.1), channel_id=1, source_target_pairs={{0,7},{1,0},{2,1},{3,2},{4,3},{5,4},{6,5},{7,6},{8,15},{9,8},{10,9... | collective-permute-start | bytes 1179656 | tf_op jit(solution)/shard_map/ppermute | solution.py:174
  27.2 5.0 %copy-start.6 = (bf16[384,512]{1,0:T(8,128)(2,1)}, bf16[384,512]{1,0:T(8,128)(2,1)S(1)}, u32[]{:S(2)}) copy-start(bf16[384,512]{1,0:T(8,128)(2,1)S(1)} %collective-permute-done) | copy-start | bytes 1179652
  27.2 10.1 %collective-permute-start.2 = (bf16[384,512]{1,0:T(8,128)(2,1)S(1)}, bf16[384,512]{1,0:T(8,128)(2,1)S(1)}, u32[]{:S(2)}, u32[]{:S(2)}) collective-permute-start(bf16[384,512]{1,0:T(8,128)(2,1)S(1)} %collective-permute-done), channel_id=1, source_target_pairs={{0,1},{1,2},{2,3},{3,4},{4,5},{5,6},{6,7},{7,0},{8,9},{9,10},{10,1... | collective-permute-start | bytes 1179656 | tf_op jit(solution)/shard_map/ppermute | solution.py:173
  37.2 17.1 %copy-start.8 = (bf16[384,512]{1,0:T(8,128)(2,1)}, bf16[384,512]{1,0:T(8,128)(2,1)S(1)}, u32[]{:S(2)}) copy-start(bf16[384,512]{1,0:T(8,128)(2,1)S(1)} %collective-permute-done.2) | copy-start | bytes 1179652
  37.2 9.2 %collective-permute-start.4 = (bf16[384,512]{1,0:T(8,128)(2,1)S(1)}, bf16[384,512]{1,0:T(8,128)(2,1)S(1)}, u32[]{:S(2)}, u32[]{:S(2)}) collective-permute-start(bf16[384,512]{1,0:T(8,128)(2,1)S(1)} %collective-permute-done.2), channel_id=1, source_target_pairs={{0,1},{1,2},{2,3},{3,4},{4,5},{5,6},{6,7},{7,0},{8,9},{9,10},{10,1... | collective-permute-start | bytes 1179656 | tf_op jit(solution)/shard_map/ppermute | solution.py:173
  37.3 12.9 %copy-start.4 = (bf16[384,512]{1,0:T(8,128)(2,1)}, bf16[384,512]{1,0:T(8,128)(2,1)S(1)}, u32[]{:S(2)}) copy-start(bf16[384,512]{1,0:T(8,128)(2,1)S(1)} %collective-permute-done.3) | copy-start | bytes 1179652
  37.3 9.3 %collective-permute-start.5 = (bf16[384,512]{1,0:T(8,128)(2,1)S(1)}, bf16[384,512]{1,0:T(8,128)(2,1)S(1)}, u32[]{:S(2)}, u32[]{:S(2)}) collective-permute-start(bf16[384,512]{1,0:T(8,128)(2,1)S(1)} %collective-permute-done.3), channel_id=1, source_target_pairs={{0,7},{1,0},{2,1},{3,2},{4,3},{5,4},{6,5},{7,6},{8,15},{9,8},{10,9... | collective-permute-start | bytes 1179656 | tf_op jit(solution)/shard_map/ppermute | solution.py:174
  46.5 5.8 %collective-permute-start.6 = (bf16[192,512]{1,0:T(8,128)(2,1)S(1)}, bf16[192,512]{1,0:T(8,128)(2,1)S(1)}, u32[]{:S(2)}, u32[]{:S(2)}) collective-permute-start(bf16[192,512]{1,0:T(8,128)(2,1)S(1)} %slice.68), channel_id=1, source_target_pairs={{0,1},{1,2},{2,3},{3,4},{4,5},{5,6},{6,7},{7,0},{8,9},{9,10},{10,1... | collective-permute-start | bytes 589832 | tf_op jit(solution)/shard_map/ppermute | solution.py:179
  46.6 5.7 %collective-permute-start.7 = (bf16[192,512]{1,0:T(8,128)(2,1)S(1)}, bf16[192,512]{1,0:T(8,128)(2,1)S(1)}, u32[]{:S(2)}, u32[]{:S(2)}) collective-permute-start(bf16[192,512]{1,0:T(8,128)(2,1)S(1)} %slice.69), channel_id=1, source_target_pairs={{0,7},{1,0},{2,1},{3,2},{4,3},{5,4},{6,5},{7,6},{8,15},{9,8},{10,9... | collective-permute-start | bytes 589832 | tf_op jit(solution)/shard_map/ppermute | solution.py:180
  52.3 0.7 copy-start.1
  64.0 4.4 %copy-start.3 = (bf16[4096,512]{1,0:T(8,128)(2,1)S(1)}, bf16[4096,512]{1,0:T(8,128)(2,1)}, u32[]{:S(2)}) copy-start(bf16[4096,512]{1,0:T(8,128)(2,1)} %param.13) | copy-start | bytes 12582916
  64.0 5.8 %copy-start.5 = (bf16[384,512]{1,0:T(8,128)(2,1)S(1)}, bf16[384,512]{1,0:T(8,128)(2,1)}, u32[]{:S(2)}) copy-start(bf16[384,512]{1,0:T(8,128)(2,1)} %copy-done.4) | copy-start | bytes 1179652
  65.2 5.0 %copy-start.9 = (bf16[384,512]{1,0:T(8,128)(2,1)S(1)}, bf16[384,512]{1,0:T(8,128)(2,1)}, u32[]{:S(2)}) copy-start(bf16[384,512]{1,0:T(8,128)(2,1)} %copy-done.8) | copy-start | bytes 1179652
  68.3 2.6 %copy-start.2 = (bf16[384,512]{1,0:T(8,128)(2,1)S(1)}, bf16[384,512]{1,0:T(8,128)(2,1)}, u32[]{:S(2)}) copy-start(bf16[384,512]{1,0:T(8,128)(2,1)} %copy-done.1) | copy-start | bytes 1179652
  72.6 53.6 %copy-start.13 = (s32[384]{0:T(512)S(1)}, s32[384]{0:T(512)}, u32[]{:S(2)}) copy-start(s32[384]{0:T(512)} %param.11) | copy-start | bytes 4612
  77.2 49.2 %copy-start.10 = (bf16[1536,128]{0,1:T(8,128)(2,1)}, bf16[1536,128]{0,1:T(8,128)(2,1)S(1)}, u32[]{:S(2)}) copy-start(bf16[1536,128]{0,1:T(8,128)(2,1)S(1)} %reshape.185) | copy-start | bytes 1179652
  77.2 49.0 %collective-permute-start.8 = (bf16[128,1536]{1,0:T(8,128)(2,1)S(1)}, bf16[128,1536]{1,0:T(8,128)(2,1)}, u32[]{:S(2)}, u32[]{:S(2)}) collective-permute-start(bf16[128,1536]{1,0:T(8,128)(2,1)S(1)} %bitcast.71), channel_id=1, source_target_pairs={{128,120},{136,112},{144,104},{152,96},{160,88},{168,80},{176,72},... | collective-permute-start | bytes 1179656 | tf_op jit(solution)/shard_map/ppermute | solution.py:237
  126.3 6.7 %copy-start.15 = (pred[384]{0:T(512)(128)(4,1)S(1)}, pred[384]{0:T(512)(128)(4,1)}, u32[]{:S(2)}) copy-start(pred[384]{0:T(512)(128)(4,1)} %copy-done.14) | copy-start | bytes 1156
  126.3 8.1 %copy-start.17 = (f32[384]{0:T(512)S(1)}, f32[384]{0:T(512)}, u32[]{:S(2)}) copy-start(f32[384]{0:T(512)} %param.12) | copy-start | bytes 4612
  127.4 40.3 %collective-permute-start.9 = (f32[136,1536]{1,0:T(8,128)}, f32[136,1536]{1,0:T(8,128)}, u32[]{:S(2)}, u32[]{:S(2)}) collective-permute-start(f32[136,1536]{1,0:T(8,128)} %get-tuple-element.49), channel_id=1, source_target_pairs={{0,248},{8,240},{16,232},{24,224},{32,216},{40,208},{48,200},{56,1... | collective-permute-start | bytes 2506760 | tf_op jit(solution)/shard_map/ppermute | solution.py:250
Sparse Core Ops, SparseCore 0:
  64.1 59.3 all-gather.1

commit v3 on v2

--- a/solution.py
+++ b/solution.py
@@ -32,7 +32,7 @@
     )
 
 
-def attend_kernel(scalars, q_ref, qpos_ref, kpos_ref, kv_ref, state_ref, *, cols, steps):
+def attend_kernel(scalars, q_ref, qpos_ref, kpos_ref, kv_ref, init_ref, state_ref, *, cols, steps):
     i = pl.program_id(0)
     first = scalars[0]
     active = i < scalars[1]
@@ -50,8 +50,7 @@
 
     @pl.when(i == 0)
     def _():
-        state_ref[...] = jnp.zeros(state_ref.shape, jnp.float32)
-        m_ref[...] = jnp.full(m_ref.shape, MASKED, jnp.float32)
+        state_ref[...] = init_ref[...]
 
     def step(qb, width, diagonal):
         c0 = qb * cols
@@ -92,7 +91,7 @@
                     step(qb, blocks * SUB, diagonal)
 
 
-def attend(scalars, q, qpos, kpos, kv, steps, interpret=False):
+def attend(scalars, q, qpos, kpos, kv, init, steps, interpret=False):
     head_dim, q_rows = q.shape
     shards, kv_rows, slots = kv.shape
     cols = kpos.shape[1]
@@ -113,6 +112,7 @@
             pl.BlockSpec((1, q_rows), fixed),
             pl.BlockSpec((slots, cols), fixed),
             pl.BlockSpec((None, SUB + head_dim, slots), shard_of),
+            pl.BlockSpec((head_dim + STATE_ROWS, q_rows), fixed),
         ],
         out_specs=pl.BlockSpec((head_dim + STATE_ROWS, q_rows), fixed),
     )
@@ -122,7 +122,13 @@
         out_shape=jax.ShapeDtypeStruct((head_dim + STATE_ROWS, q_rows), jnp.float32),
         compiler_params=pltpu.CompilerParams(dimension_semantics=("arbitrary",)),
         interpret=interpret,
-    )(scalars, q, qpos, kpos, kv)
+    )(scalars, q, qpos, kpos, kv, init)
+
+
+def empty_state(q):
+    head_dim, q_rows = q.shape
+    state = jnp.zeros((head_dim + STATE_ROWS, q_rows), jnp.float32)
+    return state.at[head_dim].set(MASKED)
 
 
 def merge(first, second):
@@ -207,6 +213,7 @@
     )
     value_rows = value_part.reshape(slot_count, kv_local, head_dim).astype(jnp.bfloat16)
     payload = pack_payload(key_rows, value_rows, live)
+    local = payload
     payload = lax.all_gather(payload, "ctx", axis=0, tiled=True)
     blocks = payload.reshape(shards, payload.shape[0] // shards, slot_count)
     flag_row = blocks.shape[1] - FLAG_ROWS
@@ -234,14 +241,21 @@
 
     own_pos = jnp.broadcast_to(chosen[:, None], (slot_count, group * SUB))
     query_pos = per_column(chosen)
-    guest_q = lax.ppermute(own_q, "ctx", [(j, shards - 1 - j) for j in range(half, shards)])
+    own_count = jnp.sum(live.astype(jnp.int32))
+    own_blocks = live_blocks(own_count)
+    diagonal_scalars = jnp.stack([0, 1, own_blocks, 0, own_count]).astype(jnp.int32)
+    diagonal_state = attend(
+        diagonal_scalars, own_q, query_pos, own_pos, local[None], empty_state(own_q), 1
+    )
+    sent_q, diagonal_state = lax.optimization_barrier((own_q, diagonal_state))
+    guest_q = lax.ppermute(sent_q, "ctx", [(j, shards - 1 - j) for j in range(half, shards)])
     guest_count = jnp.maximum(half - EXTRA_OWN - own, 0)
     guest_scalars = scalars_of(
         jnp.int32(0), guest_count, live_blocks(counts[partner]), jnp.int32(-1)
     )
 
     def guest_work(q):
-        return attend(guest_scalars, q, query_pos, own_pos, blocks, half - EXTRA_OWN)
+        return attend(guest_scalars, q, query_pos, own_pos, blocks, empty_state(q), half - EXTRA_OWN)
 
     def no_guest(q):
         return jnp.zeros((q.shape[0] + STATE_ROWS, q.shape[1]), jnp.float32)
@@ -251,9 +265,9 @@
     own_q, guest_state = lax.optimization_barrier((own_q, guest_state))
     own_first = jnp.maximum(own - (half - 1) - EXTRA_OWN, 0)
     own_scalars = scalars_of(
-        own_first, own - own_first + 1, live_blocks(jnp.sum(live.astype(jnp.int32))), own
-    )
-    own_state = attend(own_scalars, own_q, query_pos, own_pos, blocks, half + EXTRA_OWN)
+        own_first, own - own_first, own_blocks, jnp.int32(-1)
+    )
+    own_state = attend(own_scalars, own_q, query_pos, own_pos, blocks, diagonal_state, half + EXTRA_OWN - 1)
     acc, total = merge(own_state, returned)
     out = (acc / jnp.where(total > 0.0, total, 1.0)) * per_column(gated)
     out = jnp.transpose(out.astype(jnp.bfloat16))

time: 181 us -> 183 us (1.011)
  the two profiles are of different devices: /device:TPU:27 before, /device:TPU:31 now
where the time goes in v3:
time: 183 us; the launch traced here: 182 us
  waiting for transfers between devices  56.3 us (31%)
  Pallas kernels  39.3 us (21%)
  starting transfers between devices  21.8 us (12%)
  matrix products  20.2 us (11%)
  local copies, waits for them, and re-layouts  16.8 us (9%)
  between operations  15.2 us (8%)
  other arithmetic  12 us (7%)
    pallas_call x2, Pallas kernels, attend(): pl.pallas_call(kernel, grid_spec=grid_spec, out_shape=jax.ShapeDtypeStruc...  39.3 us
    all_gather x1, waiting for transfers between devices, body(): payload = lax.all_gather(payload, 'ctx', axis=0, tiled=True)  35.2 us
    dot_general x24, matrix products, partial(): jnp.dot(block, lax.dynamic_slice_in_dim(w, start, width, axis=0), preferr...  20.2 us
    ppermute x3, starting transfers between devices, ring_project(): behind = lax.ppermute(behind, axis, backward)  10.2 us
    ppermute x3, waiting for transfers between devices, ring_project(): ahead = lax.ppermute(ahead, axis, forward)  9.61 us
    ppermute x1, starting transfers between devices, body(): lax.ppermute(sent_q, 'ctx', [(j, shards - 1 - j) for j in range(half, sha...  5.38 us
    ppermute x3, waiting for transfers between devices, ring_project(): behind = lax.ppermute(behind, axis, backward)  5.03 us
    ppermute x1, waiting for transfers between devices, body(): lax.ppermute(guest_state, 'ctx', [(j, shards - 1 - j) for j in range(half)])  4.31 us
  transfers between devices with their start and end apart: 11, of which 6 were waited for; matrix products, arithmetic and copies ran while one was open for 16% of the time, Pallas kernels for 22%

profile of v3, /device:TPU:31, one launch (start us, length us, event | category | flops | bytes accessed | tf_op | source)
XLA Modules:
  0.0 181.8 jit_solution(15200920433349190339)
XLA Ops:
  8.1 2.1 %gather_fusion = bf16[384,512]{1,0:T(8,128)(2,1)S(1)} fusion(bf16[2048,512]{1,0:T(8,128)(2,1)S(1)} %copy-done, s32[1024]{0:T(1024)S(1)} %pad_clamp_fusion), kind=kCustom, calls=%fused_computation | custom fusion | bytes 787968 | tf_op jit(solution)/shard_map/gather | solution.py:205
  10.2 1.7 collective-permute-start
  11.9 4.0 %collective-permute-start.1 = (bf16[384,512]{1,0:T(8,128)(2,1)S(1)}, bf16[384,512]{1,0:T(8,128)(2,1)S(1)}, u32[]{:S(2)}, u32[]{:S(2)}) collective-permute-start(bf16[384,512]{1,0:T(8,128)(2,1)S(1)} %gather_fusion), channel_id=1, source_target_pairs={{0,7},{1,0},{2,1},{3,2},{4,3},{5,4},{6,5},{7,6},{8,15},{9,8},{10,9... | collective-permute-start | bytes 1179656 | tf_op jit(solution)/shard_map/ppermute | solution.py:180
  17.4 1.3 fusion.44
  18.7 5.0 %collective-permute-done.1 = bf16[384,512]{1,0:T(8,128)(2,1)S(1)} collective-permute-done((bf16[384,512]{1,0:T(8,128)(2,1)S(1)}, bf16[384,512]{1,0:T(8,128)(2,1)S(1)}, u32[]{:S(2)}, u32[]{:S(2)}) %collective-permute-start.1) | collective-permute-done | bytes 393248 | tf_op jit(solution)/shard_map/ppermute | solution.py:180
  23.8 3.4 %collective-permute-start.3 = (bf16[384,512]{1,0:T(8,128)(2,1)S(1)}, bf16[384,512]{1,0:T(8,128)(2,1)S(1)}, u32[]{:S(2)}, u32[]{:S(2)}) collective-permute-start(bf16[384,512]{1,0:T(8,128)(2,1)S(1)} %collective-permute-done.1), channel_id=1, source_target_pairs={{0,7},{1,0},{2,1},{3,2},{4,3},{5,4},{6,5},{7,6},{8,15},{9,8},{10,9... | collective-permute-start | bytes 1179656 | tf_op jit(solution)/shard_map/ppermute | solution.py:180
  27.2 1.4 convolution_add_fusion.11
  29.7 1.2 convolution_add_fusion.10
  32.2 5.0 %collective-permute-done.2 = bf16[384,512]{1,0:T(8,128)(2,1)S(1)} collective-permute-done((bf16[384,512]{1,0:T(8,128)(2,1)S(1)}, bf16[384,512]{1,0:T(8,128)(2,1)S(1)}, u32[]{:S(2)}, u32[]{:S(2)}) %collective-permute-start.2) | collective-permute-done | bytes 393248 | tf_op jit(solution)/shard_map/ppermute | solution.py:179
  37.3 2.7 %collective-permute-start.5 = (bf16[384,512]{1,0:T(8,128)(2,1)S(1)}, bf16[384,512]{1,0:T(8,128)(2,1)S(1)}, u32[]{:S(2)}, u32[]{:S(2)}) collective-permute-start(bf16[384,512]{1,0:T(8,128)(2,1)S(1)} %collective-permute-done.3), channel_id=1, source_target_pairs={{0,7},{1,0},{2,1},{3,2},{4,3},{5,4},{6,5},{7,6},{8,15},{9,8},{10,9... | collective-permute-start | bytes 1179656 | tf_op jit(solution)/shard_map/ppermute | solution.py:180
  41.9 4.6 %collective-permute-done.4 = bf16[384,512]{1,0:T(8,128)(2,1)S(1)} collective-permute-done((bf16[384,512]{1,0:T(8,128)(2,1)S(1)}, bf16[384,512]{1,0:T(8,128)(2,1)S(1)}, u32[]{:S(2)}, u32[]{:S(2)}) %collective-permute-start.4) | collective-permute-done | bytes 393248 | tf_op jit(solution)/shard_map/ppermute | solution.py:179
  46.6 2.9 %collective-permute-start.7 = (bf16[192,512]{1,0:T(8,128)(2,1)S(1)}, bf16[192,512]{1,0:T(8,128)(2,1)S(1)}, u32[]{:S(2)}, u32[]{:S(2)}) collective-permute-start(bf16[192,512]{1,0:T(8,128)(2,1)S(1)} %slice.97), channel_id=1, source_target_pairs={{0,7},{1,0},{2,1},{3,2},{4,3},{5,4},{6,5},{7,6},{8,15},{9,8},{10,9... | collective-permute-start | bytes 589832 | tf_op jit(solution)/shard_map/ppermute | solution.py:186
  50.1 2.2 %collective-permute-done.6 = bf16[192,512]{1,0:T(8,128)(2,1)S(1)} collective-permute-done((bf16[192,512]{1,0:T(8,128)(2,1)S(1)}, bf16[192,512]{1,0:T(8,128)(2,1)S(1)}, u32[]{:S(2)}, u32[]{:S(2)}) %collective-permute-start.6) | collective-permute-done | bytes 196640 | tf_op jit(solution)/shard_map/ppermute | solution.py:185
  56.3 1.4 concatenate.39
  59.3 1.6 copy.11
  60.9 1.4 fusion.10
  62.3 1.7 fusion.92
  67.0 1.2 multiply_cosine_fusion
  68.2 1.6 fusion.27
  69.8 1.5 convolution_add_fusion.3
  71.4 1.4 convolution_add_fusion.2
  74.3 1.3 fusion.2
  75.6 1.4 copy.16
  81.0 5.2 %shard_map.64.init_ref = f32[136,1536]{1,0:T(8,128)} custom-call(s32[5]{0:T(128)} %stack.28.scalars, bf16[128,1536]{1,0:T(8,128)(2,1)} %bitcast.72, s32[1,1536]{1,0:T(1,128)S(1)} %bitcast.79, s32[384,512]{1,0:T(8,128)S(1)} %broadcast_in_dim.55.kpos_ref, bf16[1,272,384]{2,1,0:T(8,128)(2,1)} %get-tuple-element.72.kv_ref, f32[136,1536]{1,0:T(8,128)} %constant.213.clone.1.init_ref), custom_call_target="tpu_custom_call" | custom-call | tf_op jit(solution)/shard_map/pallas_call | solution.py:119
  86.2 5.4 %collective-permute-start.8 = (bf16[128,1536]{1,0:T(8,128)(2,1)}, bf16[128,1536]{1,0:T(8,128)(2,1)S(1)}, u32[]{:S(2)}, u32[]{:S(2)}) collective-permute-start(bf16[128,1536]{1,0:T(8,128)(2,1)} %bitcast.73), channel_id=1, source_target_pairs={{128,120},{136,112},{144,104},{152,96},{160,88},{168,80},{176,72},... | collective-permute-start | bytes 1179656 | tf_op jit(solution)/shard_map/ppermute | solution.py:251
  91.6 35.2 %all-gather.2.cloned.1.call-done = bf16[8704,384]{1,0:T(8,128)(2,1)} async-done(((bf16[272,384]{1,0:T(8,128)(2,1)}), bf16[8704,384]{1,0:T(8,128)(2,1)}) %all-gather.2.cloned.1.call-update) | async-done | bytes 6684688 | tf_op jit(solution)/shard_map/all_gather | solution.py:217
  126.8 1.2 fusion.62
  129.2 1.2 conditional.1
  130.5 1.5 collective-permute-start.9
  132.7 34.2 %shard_map.65 = f32[136,1536]{1,0:T(8,128)} custom-call(s32[36]{0:T(128)} %concatenate.42.scalars, bf16[128,1536]{1,0:T(8,128)(2,1)} %bitcast.74, s32[1,1536]{1,0:T(1,128)S(1)} %bitcast.81, s32[384,512]{1,0:T(8,128)S(1)} %broadcast_in_dim.55.kpos_ref, bf16[32,272,384]{2,1,0:T(8,128)(2,1)} %bitcast.71, f32[136,1536]{1,0:T(8,128)} %shard_map.64.init_ref), custom_call_target="tpu_custom_call" | custom-call | tf_op jit(solution)/shard_map/pallas_call | solution.py:119
  166.8 4.3 %collective-permute-done.9 = f32[136,1536]{1,0:T(8,128)} collective-permute-done((f32[136,1536]{1,0:T(8,128)}, f32[136,1536]{1,0:T(8,128)}, u32[]{:S(2)}, u32[]{:S(2)}) %collective-permute-start.9) | collective-permute-done | bytes 835616 | tf_op jit(solution)/shard_map/ppermute | solution.py:264
  172.1 1.5 fusion.29
  (95 shorter events, 25.7 us)
Async XLA Ops:
  6.5 1.6 copy-start
  6.5 120.2 %all-gather.2.cloned.1.call-start = ((), (), s32[]{:S(2)}) async-start(), calls=%async_computation | async-start | bytes 6893568 | tf_op jit(solution)/shard_map/all_gather | solution.py:217
  7.4 24.8 %copy-start.13 = (pred[384]{0:T(512)(128)(4,1)}, pred[384]{0:T(512)(128)(4,1)S(1)}, u32[]{:S(2)}) copy-start(pred[384]{0:T(512)(128)(4,1)S(1)} %get-tuple-element.69) | copy-start | bytes 1156
  10.2 17.0 %collective-permute-start = (bf16[384,512]{1,0:T(8,128)(2,1)S(1)}, bf16[384,512]{1,0:T(8,128)(2,1)S(1)}, u32[]{:S(2)}, u32[]{:S(2)}) collective-permute-start(bf16[384,512]{1,0:T(8,128)(2,1)S(1)} %gather_fusion), channel_id=1, source_target_pairs={{0,1},{1,2},{2,3},{3,4},{4,5},{5,6},{6,7},{7,0},{8,9},{9,10},{10,1... | collective-permute-start | bytes 1179656 | tf_op jit(solution)/shard_map/ppermute | solution.py:179
  11.9 11.8 %collective-permute-start.1 = (bf16[384,512]{1,0:T(8,128)(2,1)S(1)}, bf16[384,512]{1,0:T(8,128)(2,1)S(1)}, u32[]{:S(2)}, u32[]{:S(2)}) collective-permute-start(bf16[384,512]{1,0:T(8,128)(2,1)S(1)} %gather_fusion), channel_id=1, source_target_pairs={{0,7},{1,0},{2,1},{3,2},{4,3},{5,4},{6,5},{7,6},{8,15},{9,8},{10,9... | collective-permute-start | bytes 1179656 | tf_op jit(solution)/shard_map/ppermute | solution.py:180
  17.2 37.2 %copy-start.15 = (f32[64]{0:T(128)}, f32[64]{0:T(128)S(1)}, u32[]{:S(2)}) copy-start(f32[64]{0:T(128)S(1)} %multiply_exponential_fusion) | copy-start | bytes 772
  17.3 22.7 %copy-start.10 = (bf16[4096,128]{1,0:T(8,128)(2,1)S(1)}, bf16[4096,128]{1,0:T(8,128)(2,1)}, u32[]{:S(2)}) copy-start(bf16[4096,128]{1,0:T(8,128)(2,1)} %param.18) | copy-start | bytes 3145732
  17.4 23.3 %copy-start.11 = (bf16[4096,128]{1,0:T(8,128)(2,1)S(1)}, bf16[4096,128]{1,0:T(8,128)(2,1)}, u32[]{:S(2)}) copy-start(bf16[4096,128]{1,0:T(8,128)(2,1)} %param.19) | copy-start | bytes 3145732
  23.7 13.5 %copy-start.7 = (bf16[384,512]{1,0:T(8,128)(2,1)}, bf16[384,512]{1,0:T(8,128)(2,1)S(1)}, u32[]{:S(2)}) copy-start(bf16[384,512]{1,0:T(8,128)(2,1)S(1)} %collective-permute-done.1) | copy-start | bytes 1179652
  23.8 13.5 %collective-permute-start.3 = (bf16[384,512]{1,0:T(8,128)(2,1)S(1)}, bf16[384,512]{1,0:T(8,128)(2,1)S(1)}, u32[]{:S(2)}, u32[]{:S(2)}) collective-permute-start(bf16[384,512]{1,0:T(8,128)(2,1)S(1)} %collective-permute-done.1), channel_id=1, source_target_pairs={{0,7},{1,0},{2,1},{3,2},{4,3},{5,4},{6,5},{7,6},{8,15},{9,8},{10,9... | collective-permute-start | bytes 1179656 | tf_op jit(solution)/shard_map/ppermute | solution.py:180
  27.2 5.0 %copy-start.6 = (bf16[384,512]{1,0:T(8,128)(2,1)}, bf16[384,512]{1,0:T(8,128)(2,1)S(1)}, u32[]{:S(2)}) copy-start(bf16[384,512]{1,0:T(8,128)(2,1)S(1)} %collective-permute-done) | copy-start | bytes 1179652
  27.2 10.1 %collective-permute-start.2 = (bf16[384,512]{1,0:T(8,128)(2,1)S(1)}, bf16[384,512]{1,0:T(8,128)(2,1)S(1)}, u32[]{:S(2)}, u32[]{:S(2)}) collective-permute-start(bf16[384,512]{1,0:T(8,128)(2,1)S(1)} %collective-permute-done), channel_id=1, source_target_pairs={{0,1},{1,2},{2,3},{3,4},{4,5},{5,6},{6,7},{7,0},{8,9},{9,10},{10,1... | collective-permute-start | bytes 1179656 | tf_op jit(solution)/shard_map/ppermute | solution.py:179
  37.2 17.1 %copy-start.8 = (bf16[384,512]{1,0:T(8,128)(2,1)}, bf16[384,512]{1,0:T(8,128)(2,1)S(1)}, u32[]{:S(2)}) copy-start(bf16[384,512]{1,0:T(8,128)(2,1)S(1)} %collective-permute-done.2) | copy-start | bytes 1179652
  37.2 9.2 %collective-permute-start.4 = (bf16[384,512]{1,0:T(8,128)(2,1)S(1)}, bf16[384,512]{1,0:T(8,128)(2,1)S(1)}, u32[]{:S(2)}, u32[]{:S(2)}) collective-permute-start(bf16[384,512]{1,0:T(8,128)(2,1)S(1)} %collective-permute-done.2), channel_id=1, source_target_pairs={{0,1},{1,2},{2,3},{3,4},{4,5},{5,6},{6,7},{7,0},{8,9},{9,10},{10,1... | collective-permute-start | bytes 1179656 | tf_op jit(solution)/shard_map/ppermute | solution.py:179
  37.3 12.9 %copy-start.4 = (bf16[384,512]{1,0:T(8,128)(2,1)}, bf16[384,512]{1,0:T(8,128)(2,1)S(1)}, u32[]{:S(2)}) copy-start(bf16[384,512]{1,0:T(8,128)(2,1)S(1)} %collective-permute-done.3) | copy-start | bytes 1179652
  37.3 9.3 %collective-permute-start.5 = (bf16[384,512]{1,0:T(8,128)(2,1)S(1)}, bf16[384,512]{1,0:T(8,128)(2,1)S(1)}, u32[]{:S(2)}, u32[]{:S(2)}) collective-permute-start(bf16[384,512]{1,0:T(8,128)(2,1)S(1)} %collective-permute-done.3), channel_id=1, source_target_pairs={{0,7},{1,0},{2,1},{3,2},{4,3},{5,4},{6,5},{7,6},{8,15},{9,8},{10,9... | collective-permute-start | bytes 1179656 | tf_op jit(solution)/shard_map/ppermute | solution.py:180
  46.5 5.8 %collective-permute-start.6 = (bf16[192,512]{1,0:T(8,128)(2,1)S(1)}, bf16[192,512]{1,0:T(8,128)(2,1)S(1)}, u32[]{:S(2)}, u32[]{:S(2)}) collective-permute-start(bf16[192,512]{1,0:T(8,128)(2,1)S(1)} %slice.96), channel_id=1, source_target_pairs={{0,1},{1,2},{2,3},{3,4},{4,5},{5,6},{6,7},{7,0},{8,9},{9,10},{10,1... | collective-permute-start | bytes 589832 | tf_op jit(solution)/shard_map/ppermute | solution.py:185
  46.6 5.7 %collective-permute-start.7 = (bf16[192,512]{1,0:T(8,128)(2,1)S(1)}, bf16[192,512]{1,0:T(8,128)(2,1)S(1)}, u32[]{:S(2)}, u32[]{:S(2)}) collective-permute-start(bf16[192,512]{1,0:T(8,128)(2,1)S(1)} %slice.97), channel_id=1, source_target_pairs={{0,7},{1,0},{2,1},{3,2},{4,3},{5,4},{6,5},{7,6},{8,15},{9,8},{10,9... | collective-permute-start | bytes 589832 | tf_op jit(solution)/shard_map/ppermute | solution.py:186
  52.3 0.7 copy-start.1
  67.0 4.4 %copy-start.3 = (bf16[4096,512]{1,0:T(8,128)(2,1)S(1)}, bf16[4096,512]{1,0:T(8,128)(2,1)}, u32[]{:S(2)}) copy-start(bf16[4096,512]{1,0:T(8,128)(2,1)} %param.17) | copy-start | bytes 12582916
  67.0 5.8 %copy-start.5 = (bf16[384,512]{1,0:T(8,128)(2,1)S(1)}, bf16[384,512]{1,0:T(8,128)(2,1)}, u32[]{:S(2)}) copy-start(bf16[384,512]{1,0:T(8,128)(2,1)} %copy-done.4) | copy-start | bytes 1179652
  68.2 4.9 %copy-start.9 = (bf16[384,512]{1,0:T(8,128)(2,1)S(1)}, bf16[384,512]{1,0:T(8,128)(2,1)}, u32[]{:S(2)}) copy-start(bf16[384,512]{1,0:T(8,128)(2,1)} %copy-done.8) | copy-start | bytes 1179652
  71.3 2.6 %copy-start.2 = (bf16[384,512]{1,0:T(8,128)(2,1)S(1)}, bf16[384,512]{1,0:T(8,128)(2,1)}, u32[]{:S(2)}) copy-start(bf16[384,512]{1,0:T(8,128)(2,1)} %copy-done.1) | copy-start | bytes 1179652
  75.6 5.3 %copy-start.12 = (s32[384]{0:T(512)S(1)}, s32[384]{0:T(512)}, u32[]{:S(2)}) copy-start(s32[384]{0:T(512)} %param.15) | copy-start | bytes 4612
  86.2 43.0 %collective-permute-start.8 = (bf16[128,1536]{1,0:T(8,128)(2,1)}, bf16[128,1536]{1,0:T(8,128)(2,1)S(1)}, u32[]{:S(2)}, u32[]{:S(2)}) collective-permute-start(bf16[128,1536]{1,0:T(8,128)(2,1)} %bitcast.73), channel_id=1, source_target_pairs={{128,120},{136,112},{144,104},{152,96},{160,88},{168,80},{176,72},... | collective-permute-start | bytes 1179656 | tf_op jit(solution)/shard_map/ppermute | solution.py:251
  129.2 2.8 %copy-start.14 = (pred[384]{0:T(512)(128)(4,1)S(1)}, pred[384]{0:T(512)(128)(4,1)}, u32[]{:S(2)}) copy-start(pred[384]{0:T(512)(128)(4,1)} %copy-done.13) | copy-start | bytes 1156
  129.2 2.8 %copy-start.16 = (f32[384]{0:T(512)S(1)}, f32[384]{0:T(512)}, u32[]{:S(2)}) copy-start(f32[384]{0:T(512)} %param.16) | copy-start | bytes 4612
  130.5 40.7 %collective-permute-start.9 = (f32[136,1536]{1,0:T(8,128)}, f32[136,1536]{1,0:T(8,128)}, u32[]{:S(2)}, u32[]{:S(2)}) collective-permute-start(f32[136,1536]{1,0:T(8,128)} %get-tuple-element.79), channel_id=1, source_target_pairs={{0,248},{8,240},{16,232},{24,224},{32,216},{40,208},{48,200},{56,1... | collective-permute-start | bytes 2506760 | tf_op jit(solution)/shard_map/ppermute | solution.py:264
Sparse Core Ops, SparseCore 0:
  64.2 62.5 all-gather.1
